TPU v7x, 32 devices: a whole 2x2x4 slice. The times are simulated.
32 devices in a mesh: row: 4 (over y, x), col: 8 (over z, core).
Axes of the slice: x: 2, y: 2, z: 4, core: 2. Of those that a mesh axis runs over, the one named last changes fastest.
Arguments:
- left_blocks: bfloat16 [96, 32, 128, 128], P('col', 'row'), may hold values from -0.5 to 0.5
- left_cols: int32 [96, 32], P('col', 'row'), may hold values from 0 to 511, as said below
- right_blocks: bfloat16 [512, 4, 128, 128], P('col', 'row'), may hold values from -6 to 6
- right_cols: int32 [512, 4], P('col', 'row'), may hold values from 0 to 127, as said below
- keep_cols: int32 [96, 16], P('col', 'row'), may hold values from 0 to 127, as said below
Outputs:
- product_blocks: bfloat16 [96, 16, 128, 128], P('col', 'row')
Inputs may be any that keep to these rules, and one draw needn't show every extreme that they name: `left_cols`: slot s of every block row names a block column in [(s // 4) * 64, (s // 4 + 1) * 64); the 4 slots of one range name distinct block columns. `right_cols`: entry [K, n] names a block column in [n * 32, (n + 1) * 32). `keep_cols`: slot k of every block row names a block column in [(k // 4) * 32, (k // 4 + 1) * 32); the 4 slots of one range name distinct block columns.
All inputs are finite; a program needn't handle non-finite values.
Results may differ from a plain program's by a relative error of at most 0.001.
Values may be sent and summed in bfloat16 or wider, within the bound.
No kernel may reach another device: no remote copies, remote signals or barrier semaphores. Data moves between devices by JAX's collectives and lax.ppermute only.
A program may use at most 192 MiB of HBM per device.

v0:
```python
import jax
import jax.numpy as jnp
from jax import lax
from jax.sharding import PartitionSpec as P

NJR = 32


def slot_index(targets, kept):
    match = targets[:, :, None] == kept[:, None, :]
    found = jnp.any(match, axis=2)
    position = jnp.sum(
        match.astype(jnp.int32) * jnp.arange(kept.shape[1], dtype=jnp.int32)[None, None, :], axis=2
    )
    return jnp.where(found, position, kept.shape[1])


def place_terms(summed, terms, targets, kept):
    index = slot_index(targets, kept)
    rows = jnp.broadcast_to(jnp.arange(terms.shape[0], dtype=jnp.int32)[:, None], index.shape)
    return summed.at[rows, index].add(terms, mode="drop")


def local(left_blocks, left_cols, right_blocks, right_cols, keep_cols):
    row_rank = lax.axis_index("row")
    kept = keep_cols - row_rank * NJR
    panel_blocks, panel_cols = (
        lax.all_gather(left_blocks, "row", axis=1, tiled=True),
        lax.all_gather(left_cols, "row", axis=1, tiled=True),
    )
    start_sum = jnp.zeros(
        (panel_blocks.shape[0], keep_cols.shape[1], panel_blocks.shape[2], panel_blocks.shape[3]),
        jnp.float32,
    )
    start = jnp.int32(0)
    piece_blocks = lax.all_gather(right_blocks, "col", axis=0, tiled=True)
    piece_cols = lax.all_gather(right_cols, "col", axis=0, tiled=True)
    local_index = panel_cols - start
    chosen = jnp.take(piece_blocks[:, 0], local_index, axis=0)
    targets = jnp.take(piece_cols[:, 0], local_index, axis=0) - row_rank * NJR
    terms = jnp.einsum("isxy,isyz->isxz", panel_blocks, chosen, preferred_element_type=jnp.float32)
    summed = place_terms(start_sum, terms, targets, kept)
    return summed.astype(jnp.bfloat16)


def solution(mesh):
    in_specs = (
        P("col", "row", None, None),
        P("col", "row"),
        P("col", "row", None, None),
        P("col", "row"),
        P("col", "row"),
    )
    out_specs = P("col", "row", None, None)
    return jax.shard_map(local, mesh=mesh, in_specs=in_specs, out_specs=out_specs, check_vma=False)
```

profile of v0, /device:TPU:0, one launch (start us, length us, event | category | flops | bytes accessed | tf_op | source)
XLA Modules:
  0.0 393.2 jit_solution(15735401039370473601)
XLA Ops:
  6.5 0.0 copy-start
  6.5 0.0 all-gather.3.cloned.1.call-start
  6.5 0.7 all-gather.3.cloned.1.call-update
  7.3 0.0 all-gather.5.cloned.1.call-start
  7.3 0.7 all-gather.5.cloned.1.call-update
  8.0 9.8 %all_gather.12 = s32[12,32]{0,1:T(8,128)S(1)} all-gather(s32[12,8]{0,1:T(8,128)} %param.6), channel_id=1, replica_groups=mesh['row'=4,'col'=8] {'row'}, dimensions={1}, use_global_device_ids=true | all-gather | bytes 1920 | tf_op jit(solution)/shard_map/all_gather | solution.py:29
  17.8 0.1 copy.21
  17.9 0.1 reshape.46
  18.0 1.2 dynamic-slice
  19.9 0.8 bitcast_dynamic-update-slice_fusion
  20.7 11.1 %all-reduce = s32[512]{0:T(512)S(1)} all-reduce(s32[512]{0:T(512)S(1)} %bitcast_dynamic-update-slice_fusion), channel_id=1, replica_groups=mesh['row'=4,'col'=8] {'col'}, use_global_device_ids=true, to_apply=%add | all-reduce | flops 512 | bytes 4096 | tf_op jit(solution)/shard_map/squeeze | solution.py:40
  31.7 2.8 gather_fusion
  34.5 0.1 reshape.45
  34.6 0.0 copy-done
  34.6 0.1 copy.24
  34.7 0.1 fusion.4
  34.8 0.1 compare_reduce_fusion
  34.9 0.1 reshape.60
  35.0 127.9 %all-gather.3.cloned.1.call-done = bf16[512,1,128,128]{3,2,1,0:T(8,128)(2,1)} async-done(((bf16[64,1,128,128]{3,2,1,0:T(8,128)(2,1)}), bf16[512,1,128,128]{3,2,1,0:T(8,128)(2,1)}) %all-gather.3.cloned.1.call-update) | async-done | bytes 16777232 | tf_op jit(solution)/shard_map/all_gather | solution.py:36
  162.9 16.8 %gather_fusion.1 = bf16[384,128,128]{2,1,0:T(8,128)(2,1)} fusion(bf16[512,128,128]{2,1,0:T(8,128)(2,1)} %bitcast.17, s32[1024]{0:T(1024)S(1)} %pad_clamp_fusion), kind=kCustom, calls=%fused_computation.1 | custom fusion | bytes 25167360 | tf_op jit(solution)/shard_map/jit(_take)/gather | solution.py:39
  179.8 16.6 %copy.25 = bf16[12,32,128,128]{2,3,1,0:T(8,128)(2,1)} copy(bf16[12,32,128,128]{3,2,1,0:T(8,128)(2,1)} %bitcast.16) | data formatting | bytes 25165824 | tf_op jit(solution)/shard_map/jit(_take)/gather | solution.py:39
  196.4 89.0 %all-gather.5.cloned.1.call-done = bf16[12,32,128,128]{3,2,1,0:T(8,128)(2,1)} async-done(((bf16[12,8,128,128]{3,2,1,0:T(8,128)(2,1)}), bf16[12,32,128,128]{3,2,1,0:T(8,128)(2,1)}) %all-gather.5.cloned.1.call-update) | async-done | bytes 12582928 | tf_op jit(solution)/shard_map/all_gather | solution.py:28
  285.4 22.1 %fusion = f32[12,32,128,128]{3,2,1,0:T(8,128)} fusion(bf16[12,32,128,128]{3,2,1,0:T(8,128)(2,1)} %all-gather.5.cloned.1.call-done, bf16[12,32,128,128]{2,3,1,0:T(8,128)(2,1)} %copy.25, pred[12,32]{1,0:T(8,128)(4,1)S(1)} %get-tuple-element.6), kind=kOutput, calls=%fused_computation.3 | convolution fusion | flops 1616904192 | bytes 50332032 | tf_op jit(solution)/shard_map/isxy,isyz->isxz/dot_general | solution.py:41
  307.5 24.7 %copy.26 = f32[384,128,128]{2,1,0:T(8,128)} copy(f32[384,128,128]{1,2,0:T(8,128)} %bitcast.15) | data formatting | bytes 50331648 | tf_op jit(solution)/shard_map/isxy,isyz->isxz/dot_general | solution.py:41
  332.2 0.4 broadcast_in_dim.38
  332.5 52.4 %scatter_fusion = f32[12,4,128,128]{3,2,1,0:T(8,128)S(1)} fusion(f32[12,4,128,128]{3,2,1,0:T(8,128)S(1)} %broadcast_in_dim.38, s32[384]{0:T(512)S(1)} %reshape.60, f32[384,128,128]{2,1,0:T(8,128)} %copy.26), kind=kCustom, calls=%fused_computation.2 | custom fusion | flops 6291456 | bytes 75500544 | tf_op jit(solution)/shard_map/scatter-add | solution.py:21
  384.9 1.4 convert_element_type.4
  (6 shorter events, 0.0 us)
Async XLA Ops:
  6.5 28.1 %copy-start = (s32[12,4]{0,1:T(4,128)S(1)}, s32[12,4]{0,1:T(4,128)}, u32[]{:S(2)}) copy-start(s32[12,4]{0,1:T(4,128)} %param.9) | copy-start | bytes 580
  6.5 156.4 %all-gather.3.cloned.1.call-start = ((), (), s32[]{:S(2)}) async-start(), calls=%async_computation | async-start | bytes 18874368 | tf_op jit(solution)/shard_map/all_gather | solution.py:36
  7.3 278.1 %all-gather.5.cloned.1.call-start = ((), (), s32[]{:S(2)}) async-start(), calls=%async_computation.1 | async-start | bytes 15728640 | tf_op jit(solution)/shard_map/all_gather | solution.py:28
Sparse Core Ops, SparseCore 0:
  8.9 153.9 all-gather.2
  164.8 120.5 all-gather.4
where the time goes:
time: 395 us; the launch traced here: 393 us
  waiting for transfers between devices  218 us (55%)
  local copies, waits for them, and re-layouts  63.7 us (16%)
  other arithmetic  54 us (14%)
  matrix products  22.1 us (6%)
  blocking collectives  20.9 us (5%)
  between operations  14.1 us (4%)
    all_gather x1, waiting for transfers between devices, local(): piece_blocks = lax.all_gather(right_blocks, 'col', axis=0, tiled=True)  128 us
    all_gather x1, waiting for transfers between devices, local(): lax.all_gather(left_blocks, 'row', axis=1, tiled=True)  89 us
    scatter-add x1, other arithmetic, place_terms(): return summed.at[rows, index].add(terms, mode='drop')  52.4 us
    gather x2, local copies, waits for them, and re-layouts, local(): chosen = jnp.take(piece_blocks[:, 0], local_index, axis=0)  33.5 us
    dot_general x1, local copies, waits for them, and re-layouts, local(): jnp.einsum('isxy,isyz->isxz', panel_blocks, chosen, preferred_element_typ...  24.7 us
    dot_general x1, matrix products, local(): jnp.einsum('isxy,isyz->isxz', panel_blocks, chosen, preferred_element_typ...  22.1 us
    squeeze x1, blocking collectives, local(): targets = jnp.take(piece_cols[:, 0], local_index, axis=0) - row_rank * NJR  11.1 us
    all_gather x1, blocking collectives, local(): lax.all_gather(left_cols, 'row', axis=1, tiled=True)  9.8 us
  transfers between devices with their start and end apart: 2, of which 2 were waited for; matrix products, arithmetic and copies ran while one was open for 10% of the time, Pallas kernels for 0%

commit v1 on v0

v1 whole, which is shorter than its diff:
```python
import jax
import jax.numpy as jnp
from jax import lax
from jax.experimental import pallas as pl
from jax.experimental.pallas import tpu as pltpu
from jax.sharding import PartitionSpec as P

NJR = 32


def kept_slot(targets, kept):
    match = targets[:, :, None] == kept[:, None, :]
    found = jnp.any(match, axis=2)
    position = jnp.sum(
        match.astype(jnp.int32) * jnp.arange(kept.shape[1], dtype=jnp.int32)[None, None, :], axis=2
    )
    return jnp.where(found, position, kept.shape[1])


def product_kernel(kidx_ref, slot_ref, left_ref, right_hbm, out_ref, rbuf, sem, acc):
    i = pl.program_id(0)
    rows = pl.num_programs(0)
    slots = left_ref.shape[0]
    kr = out_ref.shape[0]

    def fetch(row, buf):
        for s in range(slots):
            pltpu.make_async_copy(
                right_hbm.at[kidx_ref[row * slots + s]], rbuf.at[buf, s], sem.at[buf, s]
            ).start()

    @pl.when(i == 0)
    def _():
        fetch(0, 0)

    buf = i % 2

    @pl.when(i + 1 < rows)
    def _():
        fetch(i + 1, 1 - buf)

    acc[...] = jnp.zeros_like(acc)
    for s in range(slots):
        pltpu.make_async_copy(right_hbm.at[0], rbuf.at[buf, s], sem.at[buf, s]).wait()
        term = jnp.dot(left_ref[s], rbuf[buf, s], preferred_element_type=jnp.float32)
        k = slot_ref[i * slots + s]
        acc[k] += term
    out_ref[...] = acc[0:kr].astype(out_ref.dtype)


def block_product(kidx, slot, panel_blocks, right_flat, kr):
    rows, slots, bs, _ = panel_blocks.shape
    grid_spec = pltpu.PrefetchScalarGridSpec(
        num_scalar_prefetch=2,
        grid=(rows,),
        in_specs=[
            pl.BlockSpec((None, slots, bs, bs), lambda i, kidx, slot: (i, 0, 0, 0)),
            pl.BlockSpec(memory_space=pl.ANY),
        ],
        out_specs=pl.BlockSpec((None, kr, bs, bs), lambda i, kidx, slot: (i, 0, 0, 0)),
        scratch_shapes=[
            pltpu.VMEM((2, slots, bs, bs), right_flat.dtype),
            pltpu.SemaphoreType.DMA((2, slots)),
            pltpu.VMEM((kr + 1, bs, bs), jnp.float32),
        ],
    )
    flops = 2 * rows * slots * bs * bs * bs
    nbytes = 2 * (2 * rows * slots * bs * bs + rows * kr * bs * bs)
    return pl.pallas_call(
        product_kernel,
        grid_spec=grid_spec,
        out_shape=jax.ShapeDtypeStruct((rows, kr, bs, bs), jnp.bfloat16),
        compiler_params=pltpu.CompilerParams(dimension_semantics=("arbitrary",)),
        cost_estimate=pl.CostEstimate(flops=flops, transcendentals=0, bytes_accessed=nbytes),
    )(kidx, slot, panel_blocks, right_flat)


def local(left_blocks, left_cols, right_blocks, right_cols, keep_cols):
    row_rank = lax.axis_index("row")
    kept = keep_cols - row_rank * NJR
    panel_blocks = lax.all_gather(left_blocks, "row", axis=1, tiled=True)
    panel_cols = lax.all_gather(left_cols, "row", axis=1, tiled=True)
    piece_blocks = lax.all_gather(right_blocks, "col", axis=0, tiled=True)
    piece_cols = lax.all_gather(right_cols, "col", axis=0, tiled=True)
    targets = jnp.take(piece_cols[:, 0], panel_cols, axis=0) - row_rank * NJR
    slot = kept_slot(targets, kept)
    right_flat = piece_blocks[:, 0]
    return block_product(
        panel_cols.reshape(-1), slot.reshape(-1), panel_blocks, right_flat, keep_cols.shape[1]
    )


def solution(mesh):
    in_specs = (
        P("col", "row", None, None),
        P("col", "row"),
        P("col", "row", None, None),
        P("col", "row"),
        P("col", "row"),
    )
    out_specs = P("col", "row", None, None)
    return jax.shard_map(local, mesh=mesh, in_specs=in_specs, out_specs=out_specs, check_vma=False)
```

time: 395 us -> 356 us (0.901)
  Pallas kernels: 0 us -> 62.2 us
  local copies, waits for them, and re-layouts: 63.7 us -> 5.16 us
  other arithmetic: 54 us -> 0.22 us
  waiting for transfers between devices: 218 us -> 255 us
  matrix products: 22.1 us -> 0 us
    pallas_call x0 -> x1, Pallas kernels: none -> 62.2 us  [block_product(): pl.pallas_call(product_kernel, grid_spec=grid_spec, out_shape=jax.ShapeDt...]
    scatter-add x1 -> x0, other arithmetic: 52.4 us -> none  [place_terms(): return summed.at[rows, index].add(terms, mode='drop')]
    gather x4 -> x2, local copies, waits for them, and re-layouts: 36.3 us -> 2.87 us  [local(): targets = jnp.take(piece_cols[:, 0], panel_cols, axis=0) - row_rank * NJR]
    all_gather x1, waiting for transfers between devices: 128 us -> 153 us  [local(): piece_blocks = lax.all_gather(right_blocks, 'col', axis=0, tiled=True)]
    dot_general x1 -> x0, local copies, waits for them, and re-layouts: 24.7 us -> none  [local(): jnp.einsum('isxy,isyz->isxz', panel_blocks, chosen, preferred_element_typ...]
    dot_general x1 -> x0, matrix products: 22.1 us -> none  [local(): jnp.einsum('isxy,isyz->isxz', panel_blocks, chosen, preferred_element_typ...]
    all_gather x1, waiting for transfers between devices: 89 us -> 101 us  [local(): panel_blocks = lax.all_gather(left_blocks, 'row', axis=1, tiled=True)]
  transfers between devices with their start and end apart: 2 -> 2, of which waited for: 2 -> 2; matrix products, arithmetic and copies ran while one was open for 10% -> 2% of each run, Pallas kernels for 0% -> 0%
where the time goes in v1:
time: 356 us
  waiting for transfers between devices  255 us (72%)
  Pallas kernels  62.2 us (17%)
  blocking collectives  18.8 us (5%)
  between operations  14.2 us (4%)
  local copies, waits for them, and re-layouts  5.16 us (1%)
    all_gather x1, waiting for transfers between devices, local(): piece_blocks = lax.all_gather(right_blocks, 'col', axis=0, tiled=True)  153 us
    all_gather x1, waiting for transfers between devices, local(): panel_blocks = lax.all_gather(left_blocks, 'row', axis=1, tiled=True)  101 us
    pallas_call x1, Pallas kernels, block_product(): pl.pallas_call(product_kernel, grid_spec=grid_spec, out_shape=jax.ShapeDt...  62.2 us
    all_gather x1, blocking collectives, local(): panel_cols = lax.all_gather(left_cols, 'row', axis=1, tiled=True)  9.66 us
    squeeze x1, blocking collectives, local(): targets = jnp.take(piece_cols[:, 0], panel_cols, axis=0) - row_rank * NJR  9.17 us
  transfers between devices with their start and end apart: 2, of which 2 were waited for; matrix products, arithmetic and copies ran while one was open for 2% of the time, Pallas kernels for 0%

profile of v1, /device:TPU:0, one launch (start us, length us, event | category | flops | bytes accessed | tf_op | source)
XLA Modules:
  0.0 356.1 jit_solution(8199031904453584536)
XLA Ops:
  6.5 0.0 copy-start.3
  6.5 0.0 copy-start.1
  6.5 0.0 copy-start
  6.5 0.0 copy-start.2
  6.5 0.0 all-gather.3.cloned.1.call-start
  6.6 0.7 all-gather.3.cloned.1.call-update
  7.3 0.0 all-gather.5.cloned.1.call-start
  7.3 0.7 all-gather.5.cloned.1.call-update
  8.0 0.0 copy-done.1
  8.1 0.1 copy.21
  8.1 0.0 copy-done
  8.1 9.7 %all_gather.12 = s32[12,32]{0,1:T(8,128)S(1)} all-gather(s32[12,8]{0,1:T(8,128)S(1)} %copy-done), channel_id=1, replica_groups=mesh['row'=4,'col'=8] {'row'}, dimensions={1}, use_global_device_ids=true | all-gather | bytes 1920 | tf_op jit(solution)/shard_map/all_gather | solution.py:82
  17.8 0.1 copy.17
  17.9 0.7 reshape.17.kidx_ref
  18.6 0.1 reshape.20
  18.6 0.0 copy-done.3
  18.6 0.6 dynamic-slice
  19.9 0.0 copy-done.2
  19.9 0.1 bitcast_dynamic-update-slice_fusion
  20.0 9.2 %all-reduce = s32[512]{0:T(512)S(1)} all-reduce(s32[512]{0:T(512)S(1)} %bitcast_dynamic-update-slice_fusion), channel_id=1, replica_groups=mesh['row'=4,'col'=8] {'col'}, use_global_device_ids=true, to_apply=%add | all-reduce | flops 512 | bytes 4096 | tf_op jit(solution)/shard_map/squeeze | solution.py:85
  29.2 2.8 gather_fusion
  32.0 0.1 reshape.19
  32.1 0.1 compare_reduce_fusion
  32.2 0.1 fusion
  32.3 0.7 select_n.22.slot_ref
  33.0 101.4 %all-gather.3.cloned.1.call-done.left_ref = bf16[12,32,128,128]{3,2,1,0:T(8,128)(2,1)} async-done(((bf16[12,8,128,128]{3,2,1,0:T(8,128)(2,1)}), bf16[12,32,128,128]{3,2,1,0:T(8,128)(2,1)}) %all-gather.3.cloned.1.call-update) | async-done | bytes 12582928 | tf_op jit(solution)/shard_map/all_gather | solution.py:81
  134.3 152.7 %all-gather.5.cloned.1.call-done = bf16[512,1,128,128]{3,2,1,0:T(8,128)(2,1)} async-done(((bf16[64,1,128,128]{3,2,1,0:T(8,128)(2,1)}), bf16[512,1,128,128]{3,2,1,0:T(8,128)(2,1)}) %all-gather.5.cloned.1.call-update) | async-done | bytes 16777232 | tf_op jit(solution)/shard_map/all_gather | solution.py:83
  287.0 62.2 %shard_map.55 = bf16[12,4,128,128]{3,2,1,0:T(8,128)(2,1)} custom-call(s32[384]{0:T(512)} %reshape.17.kidx_ref, s32[384]{0:T(512)} %select_n.22.slot_ref, bf16[12,32,128,128]{3,2,1,0:T(8,128)(2,1)} %all-gather.3.cloned.1.call-done.left_ref, bf16[512,128,128]{2,1,0:T(8,128)(2,1)} %bitcast.4), custom_call_target="tpu_custom_call" | custom-call | flops 1610612736 | bytes 26738688 | tf_op jit(solution)/shard_map/pallas_call | solution.py:69
  (6 shorter events, 0.0 us)
Async XLA Ops:
  6.5 12.1 %copy-start.3 = (u32[32]{0:T(128)S(1)}, u32[32]{0:T(128)}, u32[]{:S(2)}) copy-start(u32[32]{0:T(128)} %constant.36) | copy-start | bytes 388
  6.5 1.5 copy-start.1
  6.5 1.6 copy-start
  6.5 13.4 %copy-start.2 = (s32[64,1]{0,1:T(1,128)S(1)}, s32[64,1]{0,1:T(1,128)}, u32[]{:S(2)}) copy-start(s32[64,1]{0,1:T(1,128)} %param.8) | copy-start | bytes 772
  6.5 127.8 %all-gather.3.cloned.1.call-start = ((), (), s32[]{:S(2)}) async-start(), calls=%async_computation | async-start | bytes 15728640 | tf_op jit(solution)/shard_map/all_gather | solution.py:81
  7.3 279.8 %all-gather.5.cloned.1.call-start = ((), (), s32[]{:S(2)}) async-start(), calls=%async_computation.1 | async-start | bytes 18874368 | tf_op jit(solution)/shard_map/all_gather | solution.py:83
Sparse Core Ops, SparseCore 0:
  9.2 125.0 all-gather.2
  135.9 151.0 all-gather.4

commit v2 on v1

v2 whole, which is shorter than its diff:
```python
import jax
import jax.numpy as jnp
from jax import lax
from jax.experimental import pallas as pl
from jax.experimental.pallas import tpu as pltpu
from jax.sharding import PartitionSpec as P

NJR = 32


def kept_slot(targets, kept):
    match = targets[:, :, None] == kept[:, None, :]
    found = jnp.any(match, axis=2)
    position = jnp.sum(
        match.astype(jnp.int32) * jnp.arange(kept.shape[1], dtype=jnp.int32)[None, None, :], axis=2
    )
    return jnp.where(found, position, kept.shape[1])


def product_kernel(table_ref, *refs):
    n_pieces = len(refs) - 6
    pieces = refs[:n_pieces]
    right_hbm = refs[n_pieces]
    out_ref, lbuf, rbuf, sem, acc_ref = refs[n_pieces + 1:]
    i = pl.program_id(0)
    rows = pl.num_programs(0)
    per_piece = pieces[0].shape[1]
    slots = n_pieces * per_piece
    kr = out_ref.shape[0]

    def fetch(row, buf):
        for s in range(slots):
            at = row * slots + s
            pos = table_ref[1, at]
            pltpu.make_async_copy(
                pieces[s // per_piece].at[row, s % per_piece], lbuf.at[buf, pos], sem.at[0, buf, s]
            ).start()
            pltpu.make_async_copy(
                right_hbm.at[table_ref[0, at]], rbuf.at[buf, pos], sem.at[1, buf, s]
            ).start()

    @pl.when(i == 0)
    def _():
        fetch(0, 0)

    buf = i % 2

    @pl.when(i + 1 < rows)
    def _():
        fetch(i + 1, 1 - buf)

    for s in range(slots):
        pltpu.make_async_copy(pieces[0].at[0, 0], lbuf.at[buf, s], sem.at[0, buf, s]).wait()
        pltpu.make_async_copy(right_hbm.at[0], rbuf.at[buf, s], sem.at[1, buf, s]).wait()

    acc_ref[...] = jnp.zeros_like(acc_ref)
    acc = None
    for j in range(slots):
        at = i * slots + j
        term = jnp.dot(lbuf[buf, j], rbuf[buf, j], preferred_element_type=jnp.float32)
        acc = term if j == 0 else jnp.where(table_ref[3, at] != 0, term, acc + term)
        acc_ref[table_ref[2, at]] = acc
    out_ref[...] = acc_ref[0:kr].astype(out_ref.dtype)


def block_product(table, pieces, right_flat, kr):
    rows, per_piece, bs, _ = pieces[0].shape
    slots = per_piece * len(pieces)
    grid_spec = pltpu.PrefetchScalarGridSpec(
        num_scalar_prefetch=1,
        grid=(rows,),
        in_specs=[pl.BlockSpec(memory_space=pl.ANY)] * (len(pieces) + 1),
        out_specs=pl.BlockSpec((None, kr, bs, bs), lambda i, table: (i, 0, 0, 0)),
        scratch_shapes=[
            pltpu.VMEM((2, slots, bs, bs), pieces[0].dtype),
            pltpu.VMEM((2, slots, bs, bs), right_flat.dtype),
            pltpu.SemaphoreType.DMA((2, 2, slots)),
            pltpu.VMEM((kr + 1, bs, bs), jnp.float32),
        ],
    )
    flops = 2 * rows * slots * bs * bs * bs
    nbytes = 2 * (2 * rows * slots * bs * bs + rows * kr * bs * bs)
    return pl.pallas_call(
        product_kernel,
        grid_spec=grid_spec,
        out_shape=jax.ShapeDtypeStruct((rows, kr, bs, bs), jnp.bfloat16),
        compiler_params=pltpu.CompilerParams(dimension_semantics=("arbitrary",)),
        cost_estimate=pl.CostEstimate(flops=flops, transcendentals=0, bytes_accessed=nbytes),
    )(table, *pieces, right_flat)


def exchange(x, axis, n):
    out = [x]
    for d in range(1, n):
        perm = [(j, j ^ d) for j in range(n)]
        out.append(lax.ppermute(x, axis, perm))
    return out


def local(left_blocks, left_cols, right_blocks, right_cols, keep_cols):
    n_row = lax.psum(1, "row")
    row_rank = lax.axis_index("row")
    kept = keep_cols - row_rank * NJR
    pieces = exchange(left_blocks, "row", n_row)
    panel_cols = jnp.concatenate(exchange(left_cols, "row", n_row), axis=1)
    piece_blocks = lax.all_gather(right_blocks, "col", axis=0, tiled=True)
    piece_cols = lax.all_gather(right_cols, "col", axis=0, tiled=True)
    targets = jnp.take(piece_cols[:, 0], panel_cols, axis=0) - row_rank * NJR
    slot = kept_slot(targets, kept)
    rows, slots = slot.shape
    order = jnp.argsort(slot, axis=1, stable=True).astype(jnp.int32)
    position = jnp.argsort(order, axis=1).astype(jnp.int32)
    sorted_slot = jnp.take_along_axis(slot, order, axis=1)
    start = jnp.concatenate(
        [jnp.ones((rows, 1), jnp.int32), (sorted_slot[:, 1:] != sorted_slot[:, :-1]).astype(jnp.int32)],
        axis=1,
    )
    table = jnp.stack([panel_cols, position, sorted_slot, start]).reshape(4, rows * slots)
    return block_product(table, pieces, piece_blocks[:, 0], keep_cols.shape[1])


def solution(mesh):
    in_specs = (
        P("col", "row", None, None),
        P("col", "row"),
        P("col", "row", None, None),
        P("col", "row"),
        P("col", "row"),
    )
    out_specs = P("col", "row", None, None)
    return jax.shard_map(local, mesh=mesh, in_specs=in_specs, out_specs=out_specs, check_vma=False)
```

time: 356 us -> 195 us (0.55)
  waiting for transfers between devices: 255 us -> 129 us
  Pallas kernels: 62.2 us -> 16.2 us
  starting transfers between devices: 0.07 us -> 9.62 us
  blocking collectives: 18.8 us -> 9.59 us
  local copies, waits for them, and re-layouts: 5.16 us -> 11.8 us
    all_gather x1, waiting for transfers between devices: 153 us -> 0.02 us  [local(): piece_blocks = lax.all_gather(right_blocks, 'col', axis=0, tiled=True)]
    ppermute x0 -> x6, waiting for transfers between devices: none -> 128 us  [exchange(): out.append(lax.ppermute(x, axis, perm))]
    all_gather x1 -> x0, waiting for transfers between devices: 101 us -> none  [local(): panel_blocks = lax.all_gather(left_blocks, 'row', axis=1, tiled=True)]
    pallas_call x1, Pallas kernels: 62.2 us -> 16.2 us  [block_product(): pl.pallas_call(product_kernel, grid_spec=grid_spec, out_shape=jax.ShapeDt...]
    all_gather x1 -> x0, blocking collectives: 9.66 us -> none  [local(): panel_cols = lax.all_gather(left_cols, 'row', axis=1, tiled=True)]
    ppermute x0 -> x6, starting transfers between devices: none -> 9.62 us  [exchange(): out.append(lax.ppermute(x, axis, perm))]
    unnamed x11 -> x6, local copies, waits for them, and re-layouts: 0.7 us -> 4.41 us
  transfers between devices with their start and end apart: 2 -> 7, of which waited for: 2 -> 1; matrix products, arithmetic and copies ran while one was open for 2% -> 7% of each run, Pallas kernels for 0% -> 0%
where the time goes in v2:
time: 195 us; the launch traced here: 194 us
  waiting for transfers between devices  129 us (66%)
  Pallas kernels  16.2 us (8%)
  between operations  14.1 us (7%)
  local copies, waits for them, and re-layouts  11.8 us (6%)
  starting transfers between devices  9.62 us (5%)
  blocking collectives  9.59 us (5%)
  other arithmetic  3.46 us (2%)
    ppermute x6, waiting for transfers between devices, exchange(): out.append(lax.ppermute(x, axis, perm))  128 us
    pallas_call x1, Pallas kernels, block_product(): pl.pallas_call(product_kernel, grid_spec=grid_spec, out_shape=jax.ShapeDt...  16.2 us
    ppermute x6, starting transfers between devices, exchange(): out.append(lax.ppermute(x, axis, perm))  9.62 us
    squeeze x1, blocking collectives, local(): targets = jnp.take(piece_cols[:, 0], panel_cols, axis=0) - row_rank * NJR  9.59 us
    unnamed x6, local copies, waits for them, and re-layouts  4.41 us
  transfers between devices with their start and end apart: 7, of which 1 were waited for; matrix products, arithmetic and copies ran while one was open for 7% of the time, Pallas kernels for 0%

profile of v2, /device:TPU:0, one launch (start us, length us, event | category | flops | bytes accessed | tf_op | source)
XLA Modules:
  0.0 193.7 jit_solution(7868143751735523058)
XLA Ops:
  6.5 0.0 all-gather.2.cloned.1.call-start
  6.5 0.7 all-gather.2.cloned.1.call-update
  7.3 3.1 %collective-permute-start.4 = (bf16[12,8,128,128]{3,2,1,0:T(8,128)(2,1)}, bf16[12,8,128,128]{3,2,1,0:T(8,128)(2,1)S(1)}, u32[]{:S(2)}, u32[]{:S(2)}) collective-permute-start(bf16[12,8,128,128]{3,2,1,0:T(8,128)(2,1)} %refs_0_.1), channel_id=1, source_target_pairs={{0,16},{8,24},{16,0},{24,8},{1,17},{9,25},{17,1},{25,9},{2,18},{10... | collective-permute-start | bytes 9437192 | tf_op jit(solution)/shard_map/ppermute | solution.py:96
  10.3 1.5 collective-permute-start.3
  11.8 0.1 collective-permute-start.5
  11.9 0.8 copy.73
  12.6 2.9 %collective-permute-start.2 = (s32[12,8]{1,0:T(8,128)S(1)}, s32[12,8]{1,0:T(8,128)S(1)}, u32[]{:S(2)}, u32[]{:S(2)}) collective-permute-start(s32[12,8]{1,0:T(8,128)S(1)} %copy.73), channel_id=1, source_target_pairs={{0,24},{8,16},{16,8},{24,0},{1,25},{9,17},{17,9},{25,1},{2,26},{10... | collective-permute-start | bytes 1160 | tf_op jit(solution)/shard_map/ppermute | solution.py:96
  15.5 0.5 collective-permute-start.1
  16.0 1.2 dynamic-slice
  17.9 0.7 broadcast_subtract_fusion
  18.6 0.7 bitcast_dynamic-update-slice_fusion
  19.3 128.1 %collective-permute-done.2 = s32[12,8]{1,0:T(8,128)S(1)} collective-permute-done((s32[12,8]{1,0:T(8,128)S(1)}, s32[12,8]{1,0:T(8,128)S(1)}, u32[]{:S(2)}, u32[]{:S(2)}) %collective-permute-start.2) | collective-permute-done | bytes 416 | tf_op jit(solution)/shard_map/ppermute | solution.py:96
  147.5 1.6 collective-permute-start
  149.1 9.6 %all-reduce.1 = s32[512]{0:T(512)S(1)} all-reduce(s32[512]{0:T(512)S(1)} %bitcast_dynamic-update-slice_fusion), channel_id=1, replica_groups=mesh['row'=4,'col'=8] {'col'}, use_global_device_ids=true, to_apply=%add.1 | all-reduce | flops 512 | bytes 4096 | tf_op jit(solution)/shard_map/squeeze | solution.py:108
  158.7 0.1 copy.81
  158.8 0.8 copy.77
  159.6 0.0 collective-permute-done.1
  159.6 0.0 collective-permute-done
  159.6 0.1 compare_select_fusion.2
  159.7 0.1 reshape.269
  159.8 2.8 %gather_fusion = s32[384]{0:T(512)S(1)} fusion(s32[512]{0:T(512)S(1)} %all-reduce.1, s32[1024]{0:T(1024)S(1)} %pad_clamp_fusion), kind=kCustom, calls=%fused_computation | custom fusion | bytes 4608 | tf_op jit(solution)/shard_map/jit(_take)/gather | solution.py:108
  162.6 0.1 reshape.268
  162.6 0.1 select_subtract_fusion
  162.7 0.1 stack.15
  162.8 0.1 compare_reduce_fusion
  162.9 0.1 fusion
  163.0 0.1 copy.82
  163.1 0.8 sort.34
  163.9 0.1 copy.84
  164.0 0.8 sort.35
  164.8 0.1 copy.83
  164.9 0.1 stack.16
  165.0 0.1 reshape.275
  165.1 2.9 %gather_fusion.1 = s32[384]{0:T(512)S(1)} fusion(s32[12,32]{1,0:T(8,128)S(1)} %broadcast_select_fusion, s32[384]{0:T(512)S(1)} %reshape.275), kind=kCustom, calls=%fused_computation.1 | custom fusion | bytes 6144 | tf_op jit(solution)/shard_map/jit(take_along_axis)/gather | solution.py:113
  167.9 0.1 reshape.278
  168.0 0.1 select_n.56
  168.1 0.1 slice_compare_fusion
  168.2 0.1 pad_convert_fusion
  168.3 0.1 reshape.266
  168.3 0.6 pad_add_fusion.1.table_ref
  168.9 0.0 collective-permute-done.4.refs_2_
  169.0 0.0 copy-start
  169.0 0.0 collective-permute-done.3.refs_1_
  169.0 0.0 collective-permute-done.5.refs_3_
  169.0 0.0 all-gather.2.cloned.1.call-done
  169.0 1.7 copy-done
  170.7 16.2 %shard_map.55 = bf16[12,4,128,128]{3,2,1,0:T(8,128)(2,1)} custom-call(s32[4,384]{1,0:T(4,128)} %pad_add_fusion.1.table_ref, bf16[12,8,128,128]{3,2,1,0:T(8,128)(2,1)} %refs_0_.1, bf16[12,8,128,128]{3,2,1,0:T(8,128)(2,1)} %collective-permute-done.3.refs_1_, bf16[12,8,128,128]{3,2,1,0:T(8,128)(2,1)} %copy-done, ...), custom_call_target="tpu_custom_call" | custom-call | flops 1610612736 | bytes 26738688 | tf_op jit(solution)/shard_map/pallas_call | solution.py:83
  (7 shorter events, 0.0 us)
Async XLA Ops:
  6.5 162.5 %all-gather.2.cloned.1.call-start = ((), (), s32[]{:S(2)}) async-start(), calls=%async_computation | async-start | bytes 18874368 | tf_op jit(solution)/shard_map/all_gather | solution.py:106
  7.3 161.7 %collective-permute-start.4 = (bf16[12,8,128,128]{3,2,1,0:T(8,128)(2,1)}, bf16[12,8,128,128]{3,2,1,0:T(8,128)(2,1)S(1)}, u32[]{:S(2)}, u32[]{:S(2)}) collective-permute-start(bf16[12,8,128,128]{3,2,1,0:T(8,128)(2,1)} %refs_0_.1), channel_id=1, source_target_pairs={{0,16},{8,24},{16,0},{24,8},{1,17},{9,25},{17,1},{25,9},{2,18},{10... | collective-permute-start | bytes 9437192 | tf_op jit(solution)/shard_map/ppermute | solution.py:96
  10.3 158.6 %collective-permute-start.3 = (bf16[12,8,128,128]{3,2,1,0:T(8,128)(2,1)}, bf16[12,8,128,128]{3,2,1,0:T(8,128)(2,1)}, u32[]{:S(2)}, u32[]{:S(2)}) collective-permute-start(bf16[12,8,128,128]{3,2,1,0:T(8,128)(2,1)} %refs_0_.1), channel_id=1, source_target_pairs={{0,8},{8,0},{16,24},{24,16},{1,9},{9,1},{17,25},{25,17},{2,10},{10... | collective-permute-start | bytes 9437192 | tf_op jit(solution)/shard_map/ppermute | solution.py:96
  11.8 157.2 %collective-permute-start.5 = (bf16[12,8,128,128]{3,2,1,0:T(8,128)(2,1)}, bf16[12,8,128,128]{3,2,1,0:T(8,128)(2,1)}, u32[]{:S(2)}, u32[]{:S(2)}) collective-permute-start(bf16[12,8,128,128]{3,2,1,0:T(8,128)(2,1)} %refs_0_.1), channel_id=1, source_target_pairs={{0,24},{8,16},{16,8},{24,0},{1,25},{9,17},{17,9},{25,1},{2,26},{10... | collective-permute-start | bytes 9437192 | tf_op jit(solution)/shard_map/ppermute | solution.py:96
  12.6 134.9 %collective-permute-start.2 = (s32[12,8]{1,0:T(8,128)S(1)}, s32[12,8]{1,0:T(8,128)S(1)}, u32[]{:S(2)}, u32[]{:S(2)}) collective-permute-start(s32[12,8]{1,0:T(8,128)S(1)} %copy.73), channel_id=1, source_target_pairs={{0,24},{8,16},{16,8},{24,0},{1,25},{9,17},{17,9},{25,1},{2,26},{10... | collective-permute-start | bytes 1160 | tf_op jit(solution)/shard_map/ppermute | solution.py:96
  15.5 144.1 %collective-permute-start.1 = (s32[12,8]{1,0:T(8,128)S(1)}, s32[12,8]{1,0:T(8,128)S(1)}, u32[]{:S(2)}, u32[]{:S(2)}) collective-permute-start(s32[12,8]{1,0:T(8,128)S(1)} %copy.73), channel_id=1, source_target_pairs={{0,16},{8,24},{16,0},{24,8},{1,17},{9,25},{17,1},{25,9},{2,18},{10... | collective-permute-start | bytes 1160 | tf_op jit(solution)/shard_map/ppermute | solution.py:96
  147.5 12.1 %collective-permute-start = (s32[12,8]{1,0:T(8,128)S(1)}, s32[12,8]{1,0:T(8,128)S(1)}, u32[]{:S(2)}, u32[]{:S(2)}) collective-permute-start(s32[12,8]{1,0:T(8,128)S(1)} %copy.73), channel_id=1, source_target_pairs={{0,8},{8,0},{16,24},{24,16},{1,9},{9,1},{17,25},{25,17},{2,10},{10... | collective-permute-start | bytes 1160 | tf_op jit(solution)/shard_map/ppermute | solution.py:96
  169.0 1.7 copy-start
Sparse Core Ops, SparseCore 0:
  8.9 154.0 all-gather.1

commit v3 on v2

v3 whole, which is shorter than its diff:
```python
import jax
import jax.numpy as jnp
from jax import lax
from jax.experimental import pallas as pl
from jax.experimental.pallas import tpu as pltpu
from jax.sharding import PartitionSpec as P

NJR = 32


def kept_slot(targets, kept):
    match = targets[:, :, None] == kept[:, None, :]
    found = jnp.any(match, axis=2)
    position = jnp.sum(
        match.astype(jnp.int32) * jnp.arange(kept.shape[1], dtype=jnp.int32)[None, None, :], axis=2
    )
    return jnp.where(found, position, kept.shape[1])


def product_kernel(table_ref, left_ref, right_hbm, out_ref, rbuf, sem, acc_ref):
    i = pl.program_id(0)
    rows = pl.num_programs(0)
    slots = left_ref.shape[0]
    kr = out_ref.shape[0]

    def fetch(row, buf):
        for s in range(slots):
            at = row * slots + s
            pltpu.make_async_copy(
                right_hbm.at[table_ref[0, at]], rbuf.at[buf, table_ref[1, at]], sem.at[buf, s]
            ).start()

    @pl.when(i == 0)
    def _():
        fetch(0, 0)

    buf = i % 2

    @pl.when(i + 1 < rows)
    def _():
        fetch(i + 1, 1 - buf)

    for s in range(slots):
        pltpu.make_async_copy(right_hbm.at[0], rbuf.at[buf, s], sem.at[buf, s]).wait()

    acc_ref[...] = jnp.zeros_like(acc_ref)
    acc = None
    for j in range(slots):
        at = i * slots + j
        term = jnp.dot(left_ref[table_ref[2, at]], rbuf[buf, j], preferred_element_type=jnp.float32)
        acc = term if j == 0 else jnp.where(table_ref[4, at] != 0, term, acc + term)
        acc_ref[table_ref[3, at]] = acc
    out_ref[...] = acc_ref[0:kr].astype(out_ref.dtype)


def block_product(table, panel, right_flat, kr):
    rows, slots, bs, _ = panel.shape
    grid_spec = pltpu.PrefetchScalarGridSpec(
        num_scalar_prefetch=1,
        grid=(rows,),
        in_specs=[
            pl.BlockSpec((None, slots, bs, bs), lambda i, table: (i, 0, 0, 0)),
            pl.BlockSpec(memory_space=pl.ANY),
        ],
        out_specs=pl.BlockSpec((None, kr, bs, bs), lambda i, table: (i, 0, 0, 0)),
        scratch_shapes=[
            pltpu.VMEM((2, slots, bs, bs), right_flat.dtype),
            pltpu.SemaphoreType.DMA((2, slots)),
            pltpu.VMEM((kr + 1, bs, bs), jnp.float32),
        ],
    )
    flops = 2 * rows * slots * bs * bs * bs
    nbytes = 2 * (2 * rows * slots * bs * bs + rows * kr * bs * bs)
    return pl.pallas_call(
        product_kernel,
        grid_spec=grid_spec,
        out_shape=jax.ShapeDtypeStruct((rows, kr, bs, bs), jnp.bfloat16),
        compiler_params=pltpu.CompilerParams(dimension_semantics=("arbitrary",)),
        cost_estimate=pl.CostEstimate(flops=flops, transcendentals=0, bytes_accessed=nbytes),
    )(table, panel, right_flat)


def exchange(x, axis, n):
    out = [x]
    for d in range(1, n):
        perm = [(j, j ^ d) for j in range(n)]
        out.append(lax.ppermute(x, axis, perm))
    return out


def local(left_blocks, left_cols, right_blocks, right_cols, keep_cols):
    n_row = lax.psum(1, "row")
    row_rank = lax.axis_index("row")
    kept = keep_cols - row_rank * NJR
    piece_blocks = lax.all_gather(right_blocks, "col", axis=0, tiled=True)
    panel_cols = jnp.concatenate(exchange(left_cols, "row", n_row), axis=1)
    left_blocks, panel_cols = lax.optimization_barrier((left_blocks, panel_cols))
    panel = jnp.concatenate(exchange(left_blocks, "row", n_row), axis=1)
    piece_cols = lax.all_gather(right_cols, "col", axis=0, tiled=True)
    targets = jnp.take(piece_cols[:, 0], panel_cols, axis=0) - row_rank * NJR
    slot = kept_slot(targets, kept)
    rows, slots = slot.shape
    order = jnp.argsort(slot, axis=1, stable=True).astype(jnp.int32)
    position = jnp.argsort(order, axis=1).astype(jnp.int32)
    sorted_slot = jnp.take_along_axis(slot, order, axis=1)
    start = jnp.concatenate(
        [jnp.ones((rows, 1), jnp.int32), (sorted_slot[:, 1:] != sorted_slot[:, :-1]).astype(jnp.int32)],
        axis=1,
    )
    table = jnp.stack([panel_cols, position, order, sorted_slot, start]).reshape(5, rows * slots)
    return block_product(table, panel, piece_blocks[:, 0], keep_cols.shape[1])


def solution(mesh):
    in_specs = (
        P("col", "row", None, None),
        P("col", "row"),
        P("col", "row", None, None),
        P("col", "row"),
        P("col", "row"),
    )
    out_specs = P("col", "row", None, None)
    return jax.shard_map(local, mesh=mesh, in_specs=in_specs, out_specs=out_specs, check_vma=False)
```

time: 195 us -> 187 us (0.959)
  waiting for transfers between devices: 129 us -> 116 us
  other arithmetic: 3.46 us -> 12.3 us
    ppermute x6, waiting for transfers between devices: 128 us -> 115 us  [exchange(): out.append(lax.ppermute(x, axis, perm))]
    concatenate x0 -> x2, other arithmetic: none -> 9.56 us  [the longest x1 9.48 us: local(): panel = jnp.concatenate(exchange(left_blocks, 'row', n_row), axis=1)]
  transfers between devices with their start and end apart: 7 -> 7, of which waited for: 1 -> 6; matrix products, arithmetic and copies ran while one was open for 7% -> 12% of each run, Pallas kernels for 0% -> 0%
where the time goes in v3:
time: 187 us; the launch traced here: 186 us
  waiting for transfers between devices  116 us (62%)
  Pallas kernels  16.4 us (9%)
  between operations  14.1 us (8%)
  other arithmetic  12.3 us (7%)
  local copies, waits for them, and re-layouts  10.1 us (5%)
  blocking collectives  9.59 us (5%)
  starting transfers between devices  7.98 us (4%)
    ppermute x6, waiting for transfers between devices, exchange(): out.append(lax.ppermute(x, axis, perm))  115 us
    pallas_call x1, Pallas kernels, block_product(): pl.pallas_call(product_kernel, grid_spec=grid_spec, out_shape=jax.ShapeDt...  16.4 us
    squeeze x1, blocking collectives, local(): targets = jnp.take(piece_cols[:, 0], panel_cols, axis=0) - row_rank * NJR  9.59 us
    concatenate x1, other arithmetic, local(): panel = jnp.concatenate(exchange(left_blocks, 'row', n_row), axis=1)  9.48 us
    ppermute x6, starting transfers between devices, exchange(): out.append(lax.ppermute(x, axis, perm))  7.98 us
  transfers between devices with their start and end apart: 7, of which 6 were waited for; matrix products, arithmetic and copies ran while one was open for 12% of the time, Pallas kernels for 0%

profile of v3, /device:TPU:0, one launch (start us, length us, event | category | flops | bytes accessed | tf_op | source)
XLA Modules:
  0.0 186.2 jit_solution(586341320026312351)
XLA Ops:
  6.5 0.0 all-gather.2.cloned.1.call-start
  6.5 0.7 all-gather.2.cloned.1.call-update
  7.3 0.8 copy.64
  8.0 3.0 %collective-permute-start = (s32[12,8]{1,0:T(8,128)S(1)}, s32[12,8]{1,0:T(8,128)S(1)}, u32[]{:S(2)}, u32[]{:S(2)}) collective-permute-start(s32[12,8]{1,0:T(8,128)S(1)} %copy.64), channel_id=1, source_target_pairs={{0,8},{8,0},{16,24},{24,16},{1,9},{9,1},{17,25},{25,17},{2,10},{10... | collective-permute-start | bytes 1160 | tf_op jit(solution)/shard_map/ppermute | solution.py:87
  11.0 1.5 collective-permute-start.1
  12.5 0.0 collective-permute-start.2
  12.5 0.1 collective-permute-done
  12.6 2.0 %collective-permute-done.1 = s32[12,8]{1,0:T(8,128)S(1)} collective-permute-done((s32[12,8]{1,0:T(8,128)S(1)}, s32[12,8]{1,0:T(8,128)S(1)}, u32[]{:S(2)}, u32[]{:S(2)}) %collective-permute-start.1) | collective-permute-done | bytes 416 | tf_op jit(solution)/shard_map/ppermute | solution.py:87
  14.6 2.4 %collective-permute-done.2 = s32[12,8]{1,0:T(8,128)S(1)} collective-permute-done((s32[12,8]{1,0:T(8,128)S(1)}, s32[12,8]{1,0:T(8,128)S(1)}, u32[]{:S(2)}, u32[]{:S(2)}) %collective-permute-start.2) | collective-permute-done | bytes 416 | tf_op jit(solution)/shard_map/ppermute | solution.py:87
  17.1 0.1 pad_add_fusion
  17.1 0.5 collective-permute-start.3
  17.7 0.1 collective-permute-start.4
  17.7 2.9 %collective-permute-start.5 = (bf16[12,8,128,128]{3,2,1,0:T(8,128)(2,1)}, bf16[12,8,128,128]{3,2,1,0:T(8,128)(2,1)}, u32[]{:S(2)}, u32[]{:S(2)}) collective-permute-start(bf16[12,8,128,128]{3,2,1,0:T(8,128)(2,1)} %param.5), channel_id=1, source_target_pairs={{0,24},{8,16},{16,8},{24,0},{1,25},{9,17},{17,9},{25,1},{2,26},{10... | collective-permute-start | bytes 9437192 | tf_op jit(solution)/shard_map/ppermute | solution.py:87
  20.6 0.7 broadcast_subtract_fusion
  21.3 0.1 copy.65
  21.4 1.2 dynamic-slice
  23.4 0.8 bitcast_dynamic-update-slice_fusion
  24.1 9.6 %all-reduce.1 = s32[512]{0:T(512)S(1)} all-reduce(s32[512]{0:T(512)S(1)} %bitcast_dynamic-update-slice_fusion), channel_id=1, replica_groups=mesh['row'=4,'col'=8] {'col'}, use_global_device_ids=true, to_apply=%add.1 | all-reduce | flops 512 | bytes 4096 | tf_op jit(solution)/shard_map/squeeze | solution.py:100
  33.7 0.1 stack.18
  33.8 0.1 reshape.55
  33.9 2.8 %gather_fusion = s32[384]{0:T(512)S(1)} fusion(s32[512]{0:T(512)S(1)} %all-reduce.1, s32[1024]{0:T(1024)S(1)} %pad_clamp_fusion), kind=kCustom, calls=%fused_computation | custom fusion | bytes 4608 | tf_op jit(solution)/shard_map/jit(_take)/gather | solution.py:100
  36.7 0.1 reshape.54
  36.8 0.1 fusion
  36.9 0.1 compare_reduce_fusion
  37.0 0.1 copy.66
  37.1 0.8 sort.34
  37.9 0.1 copy.68
  37.9 0.1 stack.20
  38.0 0.1 reshape.61
  38.1 0.0 copy-start
  38.1 2.9 %gather_fusion.1 = s32[384]{0:T(512)S(1)} fusion(s32[12,32]{1,0:T(8,128)S(1)} %broadcast_select_fusion, s32[384]{0:T(512)S(1)} %reshape.61), kind=kCustom, calls=%fused_computation.1 | custom fusion | bytes 6144 | tf_op jit(solution)/shard_map/jit(take_along_axis)/gather | solution.py:105
  41.0 0.1 reshape.64
  41.1 0.1 select_n.39
  41.2 0.1 slice_compare_fusion
  41.2 0.1 pad_convert_fusion
  41.3 0.1 reshape.52
  41.4 0.8 sort.35
  42.2 0.1 copy.67
  42.3 0.1 stack.19
  42.4 0.6 stack.23.table_ref
  43.0 45.4 %collective-permute-done.3 = bf16[12,8,128,128]{3,2,1,0:T(8,128)(2,1)} collective-permute-done((bf16[12,8,128,128]{3,2,1,0:T(8,128)(2,1)}, bf16[12,8,128,128]{3,2,1,0:T(8,128)(2,1)}, u32[]{:S(2)}, u32[]{:S(2)}) %collective-permute-start.3) | collective-permute-done | bytes 3145760 | tf_op jit(solution)/shard_map/ppermute | solution.py:87
  88.4 64.8 %collective-permute-done.4 = bf16[12,8,128,128]{3,2,1,0:T(8,128)(2,1)} collective-permute-done((bf16[12,8,128,128]{3,2,1,0:T(8,128)(2,1)}, bf16[12,8,128,128]{3,2,1,0:T(8,128)(2,1)}, u32[]{:S(2)}, u32[]{:S(2)}) %collective-permute-start.4) | collective-permute-done | bytes 3145760 | tf_op jit(solution)/shard_map/ppermute | solution.py:87
  153.3 0.0 collective-permute-done.5
  153.3 0.0 copy-done
  153.3 9.5 %pad_maximum_fusion.left_ref = bf16[12,32,128,128]{3,2,1,0:T(8,128)(2,1)} fusion(bf16[12,8,128,128]{3,2,1,0:T(8,128)(2,1)} %collective-permute-done.5, bf16[12,8,128,128]{3,2,1,0:T(8,128)(2,1)} %collective-permute-done.4, bf16[12,8,128,128]{3,2,1,0:T(8,128)(2,1)} %collective-permute-done.3, bf16[12,8,128,128]{3,2,1,0:T(8,128)(2,1)S(1)} %copy-done), kind=kLoop, calls=%fused_computation.2 | loop fusion | flops 18874368 | bytes 25165824 | tf_op jit(solution)/shard_map/concatenate | solution.py:98
  162.7 0.2 all-gather.2.cloned.1.call-done
  162.9 16.4 %shard_map.55 = bf16[12,4,128,128]{3,2,1,0:T(8,128)(2,1)} custom-call(s32[5,384]{1,0:T(8,128)} %stack.23.table_ref, bf16[12,32,128,128]{3,2,1,0:T(8,128)(2,1)} %pad_maximum_fusion.left_ref, bf16[512,128,128]{2,1,0:T(8,128)(2,1)} %bitcast.8), custom_call_target="tpu_custom_call" | custom-call | flops 1610612736 | bytes 26738688 | tf_op jit(solution)/shard_map/pallas_call | solution.py:74
  (9 shorter events, 0.1 us)
Async XLA Ops:
  6.5 156.4 %all-gather.2.cloned.1.call-start = ((), (), s32[]{:S(2)}) async-start(), calls=%async_computation | async-start | bytes 18874368 | tf_op jit(solution)/shard_map/all_gather | solution.py:95
  8.0 4.6 %collective-permute-start = (s32[12,8]{1,0:T(8,128)S(1)}, s32[12,8]{1,0:T(8,128)S(1)}, u32[]{:S(2)}, u32[]{:S(2)}) collective-permute-start(s32[12,8]{1,0:T(8,128)S(1)} %copy.64), channel_id=1, source_target_pairs={{0,8},{8,0},{16,24},{24,16},{1,9},{9,1},{17,25},{25,17},{2,10},{10... | collective-permute-start | bytes 1160 | tf_op jit(solution)/shard_map/ppermute | solution.py:87
  11.0 3.7 %collective-permute-start.1 = (s32[12,8]{1,0:T(8,128)S(1)}, s32[12,8]{1,0:T(8,128)S(1)}, u32[]{:S(2)}, u32[]{:S(2)}) collective-permute-start(s32[12,8]{1,0:T(8,128)S(1)} %copy.64), channel_id=1, source_target_pairs={{0,16},{8,24},{16,0},{24,8},{1,17},{9,25},{17,1},{25,9},{2,18},{10... | collective-permute-start | bytes 1160 | tf_op jit(solution)/shard_map/ppermute | solution.py:87
  12.5 4.5 %collective-permute-start.2 = (s32[12,8]{1,0:T(8,128)S(1)}, s32[12,8]{1,0:T(8,128)S(1)}, u32[]{:S(2)}, u32[]{:S(2)}) collective-permute-start(s32[12,8]{1,0:T(8,128)S(1)} %copy.64), channel_id=1, source_target_pairs={{0,24},{8,16},{16,8},{24,0},{1,25},{9,17},{17,9},{25,1},{2,26},{10... | collective-permute-start | bytes 1160 | tf_op jit(solution)/shard_map/ppermute | solution.py:87
  17.1 71.3 %collective-permute-start.3 = (bf16[12,8,128,128]{3,2,1,0:T(8,128)(2,1)}, bf16[12,8,128,128]{3,2,1,0:T(8,128)(2,1)}, u32[]{:S(2)}, u32[]{:S(2)}) collective-permute-start(bf16[12,8,128,128]{3,2,1,0:T(8,128)(2,1)} %param.5), channel_id=1, source_target_pairs={{0,8},{8,0},{16,24},{24,16},{1,9},{9,1},{17,25},{25,17},{2,10},{10... | collective-permute-start | bytes 9437192 | tf_op jit(solution)/shard_map/ppermute | solution.py:87
  17.7 135.6 %collective-permute-start.4 = (bf16[12,8,128,128]{3,2,1,0:T(8,128)(2,1)}, bf16[12,8,128,128]{3,2,1,0:T(8,128)(2,1)}, u32[]{:S(2)}, u32[]{:S(2)}) collective-permute-start(bf16[12,8,128,128]{3,2,1,0:T(8,128)(2,1)} %param.5), channel_id=1, source_target_pairs={{0,16},{8,24},{16,0},{24,8},{1,17},{9,25},{17,1},{25,9},{2,18},{10... | collective-permute-start | bytes 9437192 | tf_op jit(solution)/shard_map/ppermute | solution.py:87
  17.7 135.5 %collective-permute-start.5 = (bf16[12,8,128,128]{3,2,1,0:T(8,128)(2,1)}, bf16[12,8,128,128]{3,2,1,0:T(8,128)(2,1)}, u32[]{:S(2)}, u32[]{:S(2)}) collective-permute-start(bf16[12,8,128,128]{3,2,1,0:T(8,128)(2,1)} %param.5), channel_id=1, source_target_pairs={{0,24},{8,16},{16,8},{24,0},{1,25},{9,17},{17,9},{25,1},{2,26},{10... | collective-permute-start | bytes 9437192 | tf_op jit(solution)/shard_map/ppermute | solution.py:87
  38.1 115.1 %copy-start = (bf16[12,8,128,128]{3,2,1,0:T(8,128)(2,1)S(1)}, bf16[12,8,128,128]{3,2,1,0:T(8,128)(2,1)}, u32[]{:S(2)}) copy-start(bf16[12,8,128,128]{3,2,1,0:T(8,128)(2,1)} %param.5) | copy-start | bytes 9437188
Sparse Core Ops, SparseCore 0:
  8.9 153.9 all-gather.1

commit v4 on v2

v4 whole, which is shorter than its diff:
```python
import jax
import jax.numpy as jnp
from jax import lax
from jax.experimental import pallas as pl
from jax.experimental.pallas import tpu as pltpu
from jax.sharding import PartitionSpec as P

NJR = 32


def kept_slot(targets, kept):
    match = targets[:, :, None] == kept[:, None, :]
    found = jnp.any(match, axis=2)
    position = jnp.sum(
        match.astype(jnp.int32) * jnp.arange(kept.shape[1], dtype=jnp.int32)[None, None, :], axis=2
    )
    return jnp.where(found, position, kept.shape[1])


def product_kernel(table_ref, *refs):
    n_pieces = len(refs) - 7
    pieces = refs[:n_pieces]
    right_hbm, out_ref, rall, lbuf, rsem, lsem, acc_ref = refs[n_pieces:]
    i = pl.program_id(0)
    rows = pl.num_programs(0)
    per_piece = pieces[0].shape[1]
    slots = n_pieces * per_piece
    kr = out_ref.shape[0]
    n_chunks = rsem.shape[0]
    chunk = rall.shape[0] // n_chunks

    def right_copy(c):
        return pltpu.make_async_copy(
            right_hbm.at[pl.ds(c * chunk, chunk)], rall.at[pl.ds(c * chunk, chunk)], rsem.at[c]
        )

    def left_copy(row, buf, p):
        return pltpu.make_async_copy(
            pieces[p].at[row], lbuf.at[buf, pl.ds(p * per_piece, per_piece)], lsem.at[buf, p]
        )

    buf = i % 2

    @pl.when(i == 0)
    def _():
        for p in range(n_pieces):
            left_copy(0, 0, p).start()
        for c in range(n_chunks):
            right_copy(c).start()
        for c in range(n_chunks):
            right_copy(c).wait()

    @pl.when(i + 1 < rows)
    def _():
        for p in range(n_pieces):
            left_copy(i + 1, 1 - buf, p).start()

    for p in range(n_pieces):
        left_copy(0, buf, p).wait()

    acc_ref[...] = jnp.zeros_like(acc_ref)
    acc = None
    for j in range(slots):
        at = i * slots + j
        term = jnp.dot(
            lbuf[buf, table_ref[0, at]], rall[table_ref[1, at]], preferred_element_type=jnp.float32
        )
        acc = term if j == 0 else jnp.where(table_ref[3, at] != 0, term, acc + term)
        acc_ref[table_ref[2, at]] = acc
    out_ref[...] = acc_ref[0:kr].astype(out_ref.dtype)


def block_product(table, pieces, right_flat, kr):
    rows, per_piece, bs, _ = pieces[0].shape
    slots = per_piece * len(pieces)
    n_right = right_flat.shape[0]
    n_chunks = 8 if n_right % 8 == 0 else 1
    grid_spec = pltpu.PrefetchScalarGridSpec(
        num_scalar_prefetch=1,
        grid=(rows,),
        in_specs=[pl.BlockSpec(memory_space=pl.ANY)] * (len(pieces) + 1),
        out_specs=pl.BlockSpec((None, kr, bs, bs), lambda i, table: (i, 0, 0, 0)),
        scratch_shapes=[
            pltpu.VMEM((n_right, bs, bs), right_flat.dtype),
            pltpu.VMEM((2, slots, bs, bs), pieces[0].dtype),
            pltpu.SemaphoreType.DMA((n_chunks,)),
            pltpu.SemaphoreType.DMA((2, len(pieces))),
            pltpu.VMEM((kr + 1, bs, bs), jnp.float32),
        ],
    )
    flops = 2 * rows * slots * bs * bs * bs
    nbytes = 2 * (n_right * bs * bs + rows * slots * bs * bs + rows * kr * bs * bs)
    return pl.pallas_call(
        product_kernel,
        grid_spec=grid_spec,
        out_shape=jax.ShapeDtypeStruct((rows, kr, bs, bs), jnp.bfloat16),
        compiler_params=pltpu.CompilerParams(
            dimension_semantics=("arbitrary",), vmem_limit_bytes=48 * 1024 * 1024
        ),
        cost_estimate=pl.CostEstimate(flops=flops, transcendentals=0, bytes_accessed=nbytes),
    )(table, *pieces, right_flat)


def exchange(x, axis, n):
    out = [x]
    for d in range(1, n):
        perm = [(j, j ^ d) for j in range(n)]
        out.append(lax.ppermute(x, axis, perm))
    return out


def local(left_blocks, left_cols, right_blocks, right_cols, keep_cols):
    n_row = lax.psum(1, "row")
    row_rank = lax.axis_index("row")
    kept = keep_cols - row_rank * NJR
    piece_blocks = lax.all_gather(right_blocks, "col", axis=0, tiled=True)
    panel_cols = jnp.concatenate(exchange(left_cols, "row", n_row), axis=1)
    left_blocks, panel_cols = lax.optimization_barrier((left_blocks, panel_cols))
    pieces = exchange(left_blocks, "row", n_row)
    piece_cols = lax.all_gather(right_cols, "col", axis=0, tiled=True)
    targets = jnp.take(piece_cols[:, 0], panel_cols, axis=0) - row_rank * NJR
    slot = kept_slot(targets, kept)
    rows, slots = slot.shape
    order = jnp.argsort(slot, axis=1, stable=True).astype(jnp.int32)
    sorted_slot = jnp.take_along_axis(slot, order, axis=1)
    start = jnp.concatenate(
        [jnp.ones((rows, 1), jnp.int32), (sorted_slot[:, 1:] != sorted_slot[:, :-1]).astype(jnp.int32)],
        axis=1,
    )
    sorted_cols = jnp.take_along_axis(panel_cols, order, axis=1)
    table = jnp.stack([order, sorted_cols, sorted_slot, start]).reshape(4, rows * slots)
    return block_product(table, pieces, piece_blocks[:, 0], keep_cols.shape[1])


def solution(mesh):
    in_specs = (
        P("col", "row", None, None),
        P("col", "row"),
        P("col", "row", None, None),
        P("col", "row"),
        P("col", "row"),
    )
    out_specs = P("col", "row", None, None)
    return jax.shard_map(local, mesh=mesh, in_specs=in_specs, out_specs=out_specs, check_vma=False)
```

time: 195 us -> 188 us (0.964)
  waiting for transfers between devices: 129 us -> 123 us
    ppermute x6, waiting for transfers between devices: 128 us -> 113 us  [exchange(): out.append(lax.ppermute(x, axis, perm))]
    all_gather x1, waiting for transfers between devices: 0.02 us -> 9.9 us  [local(): piece_blocks = lax.all_gather(right_blocks, 'col', axis=0, tiled=True)]
    gather x0 -> x5, local copies, waits for them, and re-layouts: none -> 3.2 us  [local(): sorted_cols = jnp.take_along_axis(panel_cols, order, axis=1)]
  transfers between devices with their start and end apart: 7 -> 7, of which waited for: 1 -> 7; matrix products, arithmetic and copies ran while one was open for 7% -> 8% of each run, Pallas kernels for 0% -> 0%
where the time goes in v4:
time: 188 us; the launch traced here: 187 us
  waiting for transfers between devices  123 us (65%)
  Pallas kernels  17.5 us (9%)
  between operations  14.2 us (8%)
  local copies, waits for them, and re-layouts  12.6 us (7%)
  blocking collectives  9.71 us (5%)
  starting transfers between devices  7.98 us (4%)
  other arithmetic  2 us (1%)
    ppermute x6, waiting for transfers between devices, exchange(): out.append(lax.ppermute(x, axis, perm))  113 us
    pallas_call x1, Pallas kernels, block_product(): pl.pallas_call(product_kernel, grid_spec=grid_spec, out_shape=jax.ShapeDt...  17.5 us
    all_gather x1, waiting for transfers between devices, local(): piece_blocks = lax.all_gather(right_blocks, 'col', axis=0, tiled=True)  9.9 us
    squeeze x1, blocking collectives, local(): targets = jnp.take(piece_cols[:, 0], panel_cols, axis=0) - row_rank * NJR  9.71 us
    ppermute x6, starting transfers between devices, exchange(): out.append(lax.ppermute(x, axis, perm))  7.98 us
  transfers between devices with their start and end apart: 7, of which 7 were waited for; matrix products, arithmetic and copies ran while one was open for 8% of the time, Pallas kernels for 0%

profile of v4, /device:TPU:0, one launch (start us, length us, event | category | flops | bytes accessed | tf_op | source)
XLA Modules:
  0.0 187.3 jit_solution(465744432046471030)
XLA Ops:
  6.5 0.0 all-gather.2.cloned.1.call-start
  6.5 0.7 all-gather.2.cloned.1.call-update
  7.3 0.8 copy.78
  8.0 3.9 %collective-permute-start.2 = (s32[12,8]{1,0:T(8,128)S(1)}, s32[12,8]{1,0:T(8,128)S(1)}, u32[]{:S(2)}, u32[]{:S(2)}) collective-permute-start(s32[12,8]{1,0:T(8,128)S(1)} %copy.78), channel_id=1, source_target_pairs={{0,24},{8,16},{16,8},{24,0},{1,25},{9,17},{17,9},{25,1},{2,26},{10... | collective-permute-start | bytes 1160 | tf_op jit(solution)/shard_map/ppermute | solution.py:108
  11.9 0.5 collective-permute-start.1
  12.5 0.1 collective-permute-start
  12.5 1.1 collective-permute-done.2
  13.6 2.0 %collective-permute-done.1 = s32[12,8]{1,0:T(8,128)S(1)} collective-permute-done((s32[12,8]{1,0:T(8,128)S(1)}, s32[12,8]{1,0:T(8,128)S(1)}, u32[]{:S(2)}, u32[]{:S(2)}) %collective-permute-start.1) | collective-permute-done | bytes 416 | tf_op jit(solution)/shard_map/ppermute | solution.py:108
  15.6 0.5 collective-permute-done
  16.1 0.1 pad_add_fusion
  16.2 1.5 collective-permute-start.5
  17.7 0.1 collective-permute-start.4
  17.8 1.9 %collective-permute-start.3 = (bf16[12,8,128,128]{3,2,1,0:T(8,128)(2,1)}, bf16[12,8,128,128]{3,2,1,0:T(8,128)(2,1)}, u32[]{:S(2)}, u32[]{:S(2)}) collective-permute-start(bf16[12,8,128,128]{3,2,1,0:T(8,128)(2,1)} %refs_0_), channel_id=1, source_target_pairs={{0,8},{8,0},{16,24},{24,16},{1,9},{9,1},{17,25},{25,17},{2,10},{10... | collective-permute-start | bytes 9437192 | tf_op jit(solution)/shard_map/ppermute | solution.py:108
  19.7 0.7 broadcast_subtract_fusion
  20.4 0.1 copy.79
  20.5 1.2 dynamic-slice
  22.4 0.8 bitcast_dynamic-update-slice_fusion
  23.2 9.7 %all-reduce.1 = s32[512]{0:T(512)S(1)} all-reduce(s32[512]{0:T(512)S(1)} %bitcast_dynamic-update-slice_fusion), channel_id=1, replica_groups=mesh['row'=4,'col'=8] {'col'}, use_global_device_ids=true, to_apply=%add.1 | all-reduce | flops 512 | bytes 4096 | tf_op jit(solution)/shard_map/squeeze | solution.py:121
  32.9 0.1 reshape.43
  33.0 2.8 %gather_fusion = s32[384]{0:T(512)S(1)} fusion(s32[512]{0:T(512)S(1)} %all-reduce.1, s32[1024]{0:T(1024)S(1)} %pad_clamp_fusion), kind=kCustom, calls=%fused_computation.2 | custom fusion | bytes 4608 | tf_op jit(solution)/shard_map/jit(_take)/gather | solution.py:121
  35.8 0.1 reshape.42
  35.8 0.1 compare_reduce_fusion
  35.9 0.1 fusion
  36.1 0.1 copy.80
  36.2 0.8 sort.17
  37.0 0.1 copy.81
  37.0 0.1 stack.17
  37.1 0.1 reshape.73
  37.2 2.9 %gather_fusion.2 = s32[384]{0:T(512)S(1)} fusion(s32[12,32]{1,0:T(8,128)S(1)} %broadcast_select_fusion, s32[384]{0:T(512)S(1)} %reshape.73), kind=kCustom, calls=%fused_computation.1.clone | custom fusion | bytes 6144 | tf_op jit(solution)/shard_map/jit(take_along_axis)/gather | solution.py:125
  40.1 0.1 reshape.76
  40.2 0.1 stack.19
  40.3 0.1 slice_compare_fusion
  40.3 0.1 pad_convert_fusion
  40.4 0.1 reshape.28
  40.5 0.1 copy.82
  40.6 0.1 reshape.68
  40.7 0.0 copy-start
  40.7 2.9 %gather_fusion.1 = s32[384]{0:T(512)S(1)} fusion(s32[12,32]{1,0:T(8,128)S(1)} %pad_add_fusion, s32[384]{0:T(512)S(1)} %reshape.68), kind=kCustom, calls=%fused_computation.clone | custom fusion | bytes 6144 | tf_op jit(solution)/shard_map/jit(take_along_axis)/gather | solution.py:130
  43.6 0.1 reshape.71
  43.6 0.1 copy.83
  43.7 0.1 copy.84
  43.8 0.1 stack.18
  43.9 44.5 %collective-permute-done.5.refs_3_ = bf16[12,8,128,128]{3,2,1,0:T(8,128)(2,1)} collective-permute-done((bf16[12,8,128,128]{3,2,1,0:T(8,128)(2,1)}, bf16[12,8,128,128]{3,2,1,0:T(8,128)(2,1)}, u32[]{:S(2)}, u32[]{:S(2)}) %collective-permute-start.5) | collective-permute-done | bytes 3145760 | tf_op jit(solution)/shard_map/ppermute | solution.py:108
  88.4 64.6 %collective-permute-done.4.refs_2_ = bf16[12,8,128,128]{3,2,1,0:T(8,128)(2,1)} collective-permute-done((bf16[12,8,128,128]{3,2,1,0:T(8,128)(2,1)}, bf16[12,8,128,128]{3,2,1,0:T(8,128)(2,1)}, u32[]{:S(2)}, u32[]{:S(2)}) %collective-permute-start.4) | collective-permute-done | bytes 3145760 | tf_op jit(solution)/shard_map/ppermute | solution.py:108
  152.9 0.1 collective-permute-done.3.refs_1_
  153.0 9.9 %all-gather.2.cloned.1.call-done = bf16[512,1,128,128]{3,2,1,0:T(8,128)(2,1)} async-done(((bf16[64,1,128,128]{3,2,1,0:T(8,128)(2,1)}), bf16[512,1,128,128]{3,2,1,0:T(8,128)(2,1)}) %all-gather.2.cloned.1.call-update) | async-done | bytes 16777232 | tf_op jit(solution)/shard_map/all_gather | solution.py:116
  162.9 0.0 copy-done
  162.9 17.5 %shard_map.55 = bf16[12,4,128,128]{3,2,1,0:T(8,128)(2,1)} custom-call(s32[4,384]{1,0:T(4,128)S(1)} %pad_add_fusion.1.table_ref, bf16[12,8,128,128]{3,2,1,0:T(8,128)(2,1)S(1)} %copy-done, bf16[12,8,128,128]{3,2,1,0:T(8,128)(2,1)} %collective-permute-done.3.refs_1_, bf16[12,8,128,128]{3,2,1,0:T(8,128)(2,1)} %collective-permute-done.4.refs_2_, ...), custom_call_target="tpu_custom_call" | custom-call | flops 1610612736 | bytes 30932992 | tf_op jit(solution)/shard_map/pallas_call | solution.py:93
  (11 shorter events, 0.1 us)
Async XLA Ops:
  6.5 156.4 %all-gather.2.cloned.1.call-start = ((), (), s32[]{:S(2)}) async-start(), calls=%async_computation | async-start | bytes 18874368 | tf_op jit(solution)/shard_map/all_gather | solution.py:116
  8.0 5.6 %collective-permute-start.2 = (s32[12,8]{1,0:T(8,128)S(1)}, s32[12,8]{1,0:T(8,128)S(1)}, u32[]{:S(2)}, u32[]{:S(2)}) collective-permute-start(s32[12,8]{1,0:T(8,128)S(1)} %copy.78), channel_id=1, source_target_pairs={{0,24},{8,16},{16,8},{24,0},{1,25},{9,17},{17,9},{25,1},{2,26},{10... | collective-permute-start | bytes 1160 | tf_op jit(solution)/shard_map/ppermute | solution.py:108
  11.9 3.7 %collective-permute-start.1 = (s32[12,8]{1,0:T(8,128)S(1)}, s32[12,8]{1,0:T(8,128)S(1)}, u32[]{:S(2)}, u32[]{:S(2)}) collective-permute-start(s32[12,8]{1,0:T(8,128)S(1)} %copy.78), channel_id=1, source_target_pairs={{0,16},{8,24},{16,0},{24,8},{1,17},{9,25},{17,1},{25,9},{2,18},{10... | collective-permute-start | bytes 1160 | tf_op jit(solution)/shard_map/ppermute | solution.py:108
  12.5 3.7 %collective-permute-start = (s32[12,8]{1,0:T(8,128)S(1)}, s32[12,8]{1,0:T(8,128)S(1)}, u32[]{:S(2)}, u32[]{:S(2)}) collective-permute-start(s32[12,8]{1,0:T(8,128)S(1)} %copy.78), channel_id=1, source_target_pairs={{0,8},{8,0},{16,24},{24,16},{1,9},{9,1},{17,25},{25,17},{2,10},{10... | collective-permute-start | bytes 1160 | tf_op jit(solution)/shard_map/ppermute | solution.py:108
  16.2 72.2 %collective-permute-start.5 = (bf16[12,8,128,128]{3,2,1,0:T(8,128)(2,1)}, bf16[12,8,128,128]{3,2,1,0:T(8,128)(2,1)}, u32[]{:S(2)}, u32[]{:S(2)}) collective-permute-start(bf16[12,8,128,128]{3,2,1,0:T(8,128)(2,1)} %refs_0_), channel_id=1, source_target_pairs={{0,24},{8,16},{16,8},{24,0},{1,25},{9,17},{17,9},{25,1},{2,26},{10... | collective-permute-start | bytes 9437192 | tf_op jit(solution)/shard_map/ppermute | solution.py:108
  17.7 135.3 %collective-permute-start.4 = (bf16[12,8,128,128]{3,2,1,0:T(8,128)(2,1)}, bf16[12,8,128,128]{3,2,1,0:T(8,128)(2,1)}, u32[]{:S(2)}, u32[]{:S(2)}) collective-permute-start(bf16[12,8,128,128]{3,2,1,0:T(8,128)(2,1)} %refs_0_), channel_id=1, source_target_pairs={{0,16},{8,24},{16,0},{24,8},{1,17},{9,25},{17,1},{25,9},{2,18},{10... | collective-permute-start | bytes 9437192 | tf_op jit(solution)/shard_map/ppermute | solution.py:108
  17.8 135.3 %collective-permute-start.3 = (bf16[12,8,128,128]{3,2,1,0:T(8,128)(2,1)}, bf16[12,8,128,128]{3,2,1,0:T(8,128)(2,1)}, u32[]{:S(2)}, u32[]{:S(2)}) collective-permute-start(bf16[12,8,128,128]{3,2,1,0:T(8,128)(2,1)} %refs_0_), channel_id=1, source_target_pairs={{0,8},{8,0},{16,24},{24,16},{1,9},{9,1},{17,25},{25,17},{2,10},{10... | collective-permute-start | bytes 9437192 | tf_op jit(solution)/shard_map/ppermute | solution.py:108
  40.7 122.3 %copy-start = (bf16[12,8,128,128]{3,2,1,0:T(8,128)(2,1)S(1)}, bf16[12,8,128,128]{3,2,1,0:T(8,128)(2,1)}, u32[]{:S(2)}) copy-start(bf16[12,8,128,128]{3,2,1,0:T(8,128)(2,1)} %refs_0_) | copy-start | bytes 9437188
Sparse Core Ops, SparseCore 0:
  8.9 153.9 all-gather.1

commit v5 on v2

--- a/solution.py
+++ b/solution.py
@@ -20,24 +20,30 @@
 def product_kernel(table_ref, *refs):
     n_pieces = len(refs) - 6
     pieces = refs[:n_pieces]
-    right_hbm = refs[n_pieces]
-    out_ref, lbuf, rbuf, sem, acc_ref = refs[n_pieces + 1:]
+    right_hbm, out_ref, lbuf, rbuf, sem, acc_ref = refs[n_pieces:]
     i = pl.program_id(0)
     rows = pl.num_programs(0)
     per_piece = pieces[0].shape[1]
     slots = n_pieces * per_piece
     kr = out_ref.shape[0]
 
+    def left_copy(row, buf, s, pos):
+        return pltpu.make_async_copy(
+            pieces[s // per_piece].at[row, s % per_piece], lbuf.at[buf, pos], sem.at[0, buf, s]
+        )
+
+    def right_copy(k, buf, s, pos):
+        return pltpu.make_async_copy(right_hbm.at[k], rbuf.at[buf, pos], sem.at[1, buf, s])
+
     def fetch(row, buf):
         for s in range(slots):
             at = row * slots + s
-            pos = table_ref[1, at]
-            pltpu.make_async_copy(
-                pieces[s // per_piece].at[row, s % per_piece], lbuf.at[buf, pos], sem.at[0, buf, s]
-            ).start()
-            pltpu.make_async_copy(
-                right_hbm.at[table_ref[0, at]], rbuf.at[buf, pos], sem.at[1, buf, s]
-            ).start()
+
+            @pl.when(table_ref[2, at] != 0)
+            def _():
+                pos = table_ref[1, at]
+                left_copy(row, buf, s, pos).start()
+                right_copy(table_ref[0, at], buf, s, pos).start()
 
     @pl.when(i == 0)
     def _():
@@ -50,16 +56,20 @@
         fetch(i + 1, 1 - buf)
 
     for s in range(slots):
-        pltpu.make_async_copy(pieces[0].at[0, 0], lbuf.at[buf, s], sem.at[0, buf, s]).wait()
-        pltpu.make_async_copy(right_hbm.at[0], rbuf.at[buf, s], sem.at[1, buf, s]).wait()
+        at = i * slots + s
+
+        @pl.when(table_ref[2, at] != 0)
+        def _():
+            left_copy(0, buf, s, s).wait()
+            right_copy(0, buf, s, s).wait()
 
     acc_ref[...] = jnp.zeros_like(acc_ref)
     acc = None
     for j in range(slots):
         at = i * slots + j
         term = jnp.dot(lbuf[buf, j], rbuf[buf, j], preferred_element_type=jnp.float32)
-        acc = term if j == 0 else jnp.where(table_ref[3, at] != 0, term, acc + term)
-        acc_ref[table_ref[2, at]] = acc
+        acc = term if j == 0 else jnp.where(table_ref[4, at] != 0, term, acc + term)
+        acc_ref[table_ref[3, at]] = acc
     out_ref[...] = acc_ref[0:kr].astype(out_ref.dtype)
 
 
@@ -101,21 +111,23 @@
     n_row = lax.psum(1, "row")
     row_rank = lax.axis_index("row")
     kept = keep_cols - row_rank * NJR
+    piece_blocks = lax.all_gather(right_blocks, "col", axis=0, tiled=True)
+    panel_cols = jnp.concatenate(exchange(left_cols, "row", n_row), axis=1)
+    left_blocks, panel_cols = lax.optimization_barrier((left_blocks, panel_cols))
     pieces = exchange(left_blocks, "row", n_row)
-    panel_cols = jnp.concatenate(exchange(left_cols, "row", n_row), axis=1)
-    piece_blocks = lax.all_gather(right_blocks, "col", axis=0, tiled=True)
     piece_cols = lax.all_gather(right_cols, "col", axis=0, tiled=True)
     targets = jnp.take(piece_cols[:, 0], panel_cols, axis=0) - row_rank * NJR
     slot = kept_slot(targets, kept)
     rows, slots = slot.shape
     order = jnp.argsort(slot, axis=1, stable=True).astype(jnp.int32)
-    position = jnp.argsort(order, axis=1).astype(jnp.int32)
     sorted_slot = jnp.take_along_axis(slot, order, axis=1)
     start = jnp.concatenate(
         [jnp.ones((rows, 1), jnp.int32), (sorted_slot[:, 1:] != sorted_slot[:, :-1]).astype(jnp.int32)],
         axis=1,
     )
-    table = jnp.stack([panel_cols, position, sorted_slot, start]).reshape(4, rows * slots)
+    position = jnp.argsort(order, axis=1).astype(jnp.int32)
+    used = (slot < keep_cols.shape[1]).astype(jnp.int32)
+    table = jnp.stack([panel_cols, position, used, sorted_slot, start]).reshape(5, rows * slots)
     return block_product(table, pieces, piece_blocks[:, 0], keep_cols.shape[1])
 
 

time: 195 us -> 186 us (0.954)
  waiting for transfers between devices: 129 us -> 125 us
    ppermute x6, waiting for transfers between devices: 128 us -> 114 us  [exchange(): out.append(lax.ppermute(x, axis, perm))]
    all_gather x1, waiting for transfers between devices: 0.02 us -> 9.89 us  [local(): piece_blocks = lax.all_gather(right_blocks, 'col', axis=0, tiled=True)]
  transfers between devices with their start and end apart: 7 -> 7, of which waited for: 1 -> 7; matrix products, arithmetic and copies ran while one was open for 7% -> 7% of each run, Pallas kernels for 0% -> 0%
where the time goes in v5:
time: 186 us; the launch traced here: 185 us
  waiting for transfers between devices  125 us (67%)
  Pallas kernels  15.3 us (8%)
  between operations  14.1 us (8%)
  local copies, waits for them, and re-layouts  10.1 us (5%)
  blocking collectives  9.71 us (5%)
  starting transfers between devices  7.98 us (4%)
  other arithmetic  2.77 us (1%)
    ppermute x6, waiting for transfers between devices, exchange(): out.append(lax.ppermute(x, axis, perm))  114 us
    pallas_call x1, Pallas kernels, block_product(): pl.pallas_call(product_kernel, grid_spec=grid_spec, out_shape=jax.ShapeDt...  15.3 us
    all_gather x1, waiting for transfers between devices, local(): piece_blocks = lax.all_gather(right_blocks, 'col', axis=0, tiled=True)  9.89 us
    squeeze x1, blocking collectives, local(): targets = jnp.take(piece_cols[:, 0], panel_cols, axis=0) - row_rank * NJR  9.71 us
    ppermute x6, starting transfers between devices, exchange(): out.append(lax.ppermute(x, axis, perm))  7.98 us
  transfers between devices with their start and end apart: 7, of which 7 were waited for; matrix products, arithmetic and copies ran while one was open for 7% of the time, Pallas kernels for 0%

profile of v5, /device:TPU:0, one launch (start us, length us, event | category | flops | bytes accessed | tf_op | source)
XLA Modules:
  0.0 185.2 jit_solution(3331143552732001171)
XLA Ops:
  6.5 0.0 all-gather.2.cloned.1.call-start
  6.5 0.7 all-gather.2.cloned.1.call-update
  7.3 0.8 copy.63
  8.0 3.9 %collective-permute-start.2 = (s32[12,8]{1,0:T(8,128)S(1)}, s32[12,8]{1,0:T(8,128)S(1)}, u32[]{:S(2)}, u32[]{:S(2)}) collective-permute-start(s32[12,8]{1,0:T(8,128)S(1)} %copy.63), channel_id=1, source_target_pairs={{0,24},{8,16},{16,8},{24,0},{1,25},{9,17},{17,9},{25,1},{2,26},{10... | collective-permute-start | bytes 1160 | tf_op jit(solution)/shard_map/ppermute | solution.py:106
  11.9 0.5 collective-permute-start.1
  12.5 0.1 collective-permute-start
  12.5 1.1 collective-permute-done.2
  13.6 2.0 %collective-permute-done.1 = s32[12,8]{1,0:T(8,128)S(1)} collective-permute-done((s32[12,8]{1,0:T(8,128)S(1)}, s32[12,8]{1,0:T(8,128)S(1)}, u32[]{:S(2)}, u32[]{:S(2)}) %collective-permute-start.1) | collective-permute-done | bytes 416 | tf_op jit(solution)/shard_map/ppermute | solution.py:106
  15.6 0.5 collective-permute-done
  16.1 0.1 pad_add_fusion
  16.2 1.5 collective-permute-start.5
  17.7 0.1 collective-permute-start.4
  17.8 1.9 %collective-permute-start.3 = (bf16[12,8,128,128]{3,2,1,0:T(8,128)(2,1)}, bf16[12,8,128,128]{3,2,1,0:T(8,128)(2,1)}, u32[]{:S(2)}, u32[]{:S(2)}) collective-permute-start(bf16[12,8,128,128]{3,2,1,0:T(8,128)(2,1)} %refs_0_), channel_id=1, source_target_pairs={{0,8},{8,0},{16,24},{24,16},{1,9},{9,1},{17,25},{25,17},{2,10},{10... | collective-permute-start | bytes 9437192 | tf_op jit(solution)/shard_map/ppermute | solution.py:106
  19.7 0.7 broadcast_subtract_fusion
  20.4 0.1 copy.64
  20.5 1.2 dynamic-slice
  22.4 0.8 bitcast_dynamic-update-slice_fusion
  23.2 9.7 %all-reduce.1 = s32[512]{0:T(512)S(1)} all-reduce(s32[512]{0:T(512)S(1)} %bitcast_dynamic-update-slice_fusion), channel_id=1, replica_groups=mesh['row'=4,'col'=8] {'col'}, use_global_device_ids=true, to_apply=%add.1 | all-reduce | flops 512 | bytes 4096 | tf_op jit(solution)/shard_map/squeeze | solution.py:119
  32.9 0.1 stack.16
  33.0 0.1 reshape.86
  33.0 2.8 %gather_fusion = s32[384]{0:T(512)S(1)} fusion(s32[512]{0:T(512)S(1)} %all-reduce.1, s32[1024]{0:T(1024)S(1)} %pad_clamp_fusion), kind=kCustom, calls=%fused_computation | custom fusion | bytes 4608 | tf_op jit(solution)/shard_map/jit(_take)/gather | solution.py:119
  35.8 0.1 reshape.85
  35.9 0.1 compare_reduce_fusion
  36.0 0.1 fusion
  36.1 0.1 reshape.82
  36.2 0.1 copy.65
  36.3 0.8 sort.34
  37.1 0.1 copy.67
  37.2 0.8 sort.35
  38.0 0.1 copy.66
  38.1 0.1 stack.17
  38.2 0.1 reshape.92
  38.3 2.9 %gather_fusion.1 = s32[384]{0:T(512)S(1)} fusion(s32[12,32]{1,0:T(8,128)S(1)} %get-tuple-element.14, s32[384]{0:T(512)S(1)} %reshape.92), kind=kCustom, calls=%fused_computation.1 | custom fusion | bytes 6144 | tf_op jit(solution)/shard_map/jit(take_along_axis)/gather | solution.py:123
  41.1 0.1 reshape.95
  41.2 0.1 select_n.48
  41.3 0.1 slice_compare_fusion
  41.4 0.1 pad_convert_fusion
  41.5 0.1 reshape.83
  41.5 0.6 stack.20.table_ref
  42.2 46.1 %collective-permute-done.5.refs_3_ = bf16[12,8,128,128]{3,2,1,0:T(8,128)(2,1)S(1)} collective-permute-done((bf16[12,8,128,128]{3,2,1,0:T(8,128)(2,1)}, bf16[12,8,128,128]{3,2,1,0:T(8,128)(2,1)S(1)}, u32[]{:S(2)}, u32[]{:S(2)}) %collective-permute-start.5) | collective-permute-done | bytes 3145760 | tf_op jit(solution)/shard_map/ppermute | solution.py:106
  88.3 0.0 copy-start
  88.3 64.7 %collective-permute-done.4.refs_2_ = bf16[12,8,128,128]{3,2,1,0:T(8,128)(2,1)} collective-permute-done((bf16[12,8,128,128]{3,2,1,0:T(8,128)(2,1)}, bf16[12,8,128,128]{3,2,1,0:T(8,128)(2,1)}, u32[]{:S(2)}, u32[]{:S(2)}) %collective-permute-start.4) | collective-permute-done | bytes 3145760 | tf_op jit(solution)/shard_map/ppermute | solution.py:106
  152.9 0.1 collective-permute-done.3.refs_1_
  153.1 9.9 %all-gather.2.cloned.1.call-done = bf16[512,1,128,128]{3,2,1,0:T(8,128)(2,1)} async-done(((bf16[64,1,128,128]{3,2,1,0:T(8,128)(2,1)}), bf16[512,1,128,128]{3,2,1,0:T(8,128)(2,1)}) %all-gather.2.cloned.1.call-update) | async-done | bytes 16777232 | tf_op jit(solution)/shard_map/all_gather | solution.py:114
  162.9 0.0 copy-done
  162.9 15.3 %shard_map.55 = bf16[12,4,128,128]{3,2,1,0:T(8,128)(2,1)} custom-call(s32[5,384]{1,0:T(8,128)} %stack.20.table_ref, bf16[12,8,128,128]{3,2,1,0:T(8,128)(2,1)} %refs_0_, bf16[12,8,128,128]{3,2,1,0:T(8,128)(2,1)} %collective-permute-done.3.refs_1_, bf16[12,8,128,128]{3,2,1,0:T(8,128)(2,1)} %collective-permute-done.4.refs_2_, ...), custom_call_target="tpu_custom_call" | custom-call | flops 1610612736 | bytes 26738688 | tf_op jit(solution)/shard_map/pallas_call | solution.py:93
  (9 shorter events, 0.1 us)
Async XLA Ops:
  6.5 156.4 %all-gather.2.cloned.1.call-start = ((), (), s32[]{:S(2)}) async-start(), calls=%async_computation | async-start | bytes 18874368 | tf_op jit(solution)/shard_map/all_gather | solution.py:114
  8.0 5.6 %collective-permute-start.2 = (s32[12,8]{1,0:T(8,128)S(1)}, s32[12,8]{1,0:T(8,128)S(1)}, u32[]{:S(2)}, u32[]{:S(2)}) collective-permute-start(s32[12,8]{1,0:T(8,128)S(1)} %copy.63), channel_id=1, source_target_pairs={{0,24},{8,16},{16,8},{24,0},{1,25},{9,17},{17,9},{25,1},{2,26},{10... | collective-permute-start | bytes 1160 | tf_op jit(solution)/shard_map/ppermute | solution.py:106
  11.9 3.7 %collective-permute-start.1 = (s32[12,8]{1,0:T(8,128)S(1)}, s32[12,8]{1,0:T(8,128)S(1)}, u32[]{:S(2)}, u32[]{:S(2)}) collective-permute-start(s32[12,8]{1,0:T(8,128)S(1)} %copy.63), channel_id=1, source_target_pairs={{0,16},{8,24},{16,0},{24,8},{1,17},{9,25},{17,1},{25,9},{2,18},{10... | collective-permute-start | bytes 1160 | tf_op jit(solution)/shard_map/ppermute | solution.py:106
  12.5 3.7 %collective-permute-start = (s32[12,8]{1,0:T(8,128)S(1)}, s32[12,8]{1,0:T(8,128)S(1)}, u32[]{:S(2)}, u32[]{:S(2)}) collective-permute-start(s32[12,8]{1,0:T(8,128)S(1)} %copy.63), channel_id=1, source_target_pairs={{0,8},{8,0},{16,24},{24,16},{1,9},{9,1},{17,25},{25,17},{2,10},{10... | collective-permute-start | bytes 1160 | tf_op jit(solution)/shard_map/ppermute | solution.py:106
  16.2 72.1 %collective-permute-start.5 = (bf16[12,8,128,128]{3,2,1,0:T(8,128)(2,1)}, bf16[12,8,128,128]{3,2,1,0:T(8,128)(2,1)S(1)}, u32[]{:S(2)}, u32[]{:S(2)}) collective-permute-start(bf16[12,8,128,128]{3,2,1,0:T(8,128)(2,1)} %refs_0_), channel_id=1, source_target_pairs={{0,24},{8,16},{16,8},{24,0},{1,25},{9,17},{17,9},{25,1},{2,26},{10... | collective-permute-start | bytes 9437192 | tf_op jit(solution)/shard_map/ppermute | solution.py:106
  17.7 135.3 %collective-permute-start.4 = (bf16[12,8,128,128]{3,2,1,0:T(8,128)(2,1)}, bf16[12,8,128,128]{3,2,1,0:T(8,128)(2,1)}, u32[]{:S(2)}, u32[]{:S(2)}) collective-permute-start(bf16[12,8,128,128]{3,2,1,0:T(8,128)(2,1)} %refs_0_), channel_id=1, source_target_pairs={{0,16},{8,24},{16,0},{24,8},{1,17},{9,25},{17,1},{25,9},{2,18},{10... | collective-permute-start | bytes 9437192 | tf_op jit(solution)/shard_map/ppermute | solution.py:106
  17.8 135.3 %collective-permute-start.3 = (bf16[12,8,128,128]{3,2,1,0:T(8,128)(2,1)}, bf16[12,8,128,128]{3,2,1,0:T(8,128)(2,1)}, u32[]{:S(2)}, u32[]{:S(2)}) collective-permute-start(bf16[12,8,128,128]{3,2,1,0:T(8,128)(2,1)} %refs_0_), channel_id=1, source_target_pairs={{0,8},{8,0},{16,24},{24,16},{1,9},{9,1},{17,25},{25,17},{2,10},{10... | collective-permute-start | bytes 9437192 | tf_op jit(solution)/shard_map/ppermute | solution.py:106
  88.3 74.7 %copy-start = (bf16[12,8,128,128]{3,2,1,0:T(8,128)(2,1)}, bf16[12,8,128,128]{3,2,1,0:T(8,128)(2,1)S(1)}, u32[]{:S(2)}) copy-start(bf16[12,8,128,128]{3,2,1,0:T(8,128)(2,1)S(1)} %collective-permute-done.5.refs_3_) | copy-start | bytes 9437188
Sparse Core Ops, SparseCore 0:
  8.9 153.9 all-gather.1

commit v6 on v5

--- a/solution.py
+++ b/solution.py
@@ -6,6 +6,7 @@
 from jax.sharding import PartitionSpec as P
 
 NJR = 32
+CHUNK = 4
 
 
 def kept_slot(targets, kept):
@@ -18,9 +19,9 @@
 
 
 def product_kernel(table_ref, *refs):
-    n_pieces = len(refs) - 6
+    n_pieces = len(refs) - 7
     pieces = refs[:n_pieces]
-    right_hbm, out_ref, lbuf, rbuf, sem, acc_ref = refs[n_pieces:]
+    right_hbm, out_ref, lbuf, rbuf, sem, acc_ref, carry_ref = refs[n_pieces:]
     i = pl.program_id(0)
     rows = pl.num_programs(0)
     per_piece = pieces[0].shape[1]
@@ -64,12 +65,19 @@
             right_copy(0, buf, s, s).wait()
 
     acc_ref[...] = jnp.zeros_like(acc_ref)
-    acc = None
-    for j in range(slots):
-        at = i * slots + j
-        term = jnp.dot(lbuf[buf, j], rbuf[buf, j], preferred_element_type=jnp.float32)
-        acc = term if j == 0 else jnp.where(table_ref[4, at] != 0, term, acc + term)
-        acc_ref[table_ref[3, at]] = acc
+    n_used = table_ref[5, i * slots]
+    for c in range(0, slots, CHUNK):
+
+        @pl.when(c < n_used)
+        def _():
+            acc = None if c == 0 else carry_ref[...]
+            for j in range(c, min(c + CHUNK, slots)):
+                at = i * slots + j
+                term = jnp.dot(lbuf[buf, j], rbuf[buf, j], preferred_element_type=jnp.float32)
+                acc = term if j == 0 else jnp.where(table_ref[4, at] != 0, term, acc + term)
+                acc_ref[table_ref[3, at]] = acc
+            carry_ref[...] = acc
+
     out_ref[...] = acc_ref[0:kr].astype(out_ref.dtype)
 
 
@@ -86,6 +94,7 @@
             pltpu.VMEM((2, slots, bs, bs), right_flat.dtype),
             pltpu.SemaphoreType.DMA((2, 2, slots)),
             pltpu.VMEM((kr + 1, bs, bs), jnp.float32),
+            pltpu.VMEM((bs, bs), jnp.float32),
         ],
     )
     flops = 2 * rows * slots * bs * bs * bs
@@ -127,7 +136,8 @@
     )
     position = jnp.argsort(order, axis=1).astype(jnp.int32)
     used = (slot < keep_cols.shape[1]).astype(jnp.int32)
-    table = jnp.stack([panel_cols, position, used, sorted_slot, start]).reshape(5, rows * slots)
+    n_used = jnp.broadcast_to(jnp.sum(used, axis=1, keepdims=True), (rows, slots))
+    table = jnp.stack([panel_cols, position, used, sorted_slot, start, n_used]).reshape(6, rows * slots)
     return block_product(table, pieces, piece_blocks[:, 0], keep_cols.shape[1])
 
 

time: 186 us -> 189 us (1.016)
  Pallas kernels: 15.3 us -> 18.3 us
    pallas_call x1, Pallas kernels: 15.3 us -> 18.3 us  [block_product(): pl.pallas_call(product_kernel, grid_spec=grid_spec, out_shape=jax.ShapeDt...]
where the time goes in v6:
time: 189 us; the launch traced here: 188 us
  waiting for transfers between devices  125 us (66%)
  Pallas kernels  18.3 us (10%)
  between operations  14.1 us (7%)
  local copies, waits for them, and re-layouts  10.3 us (5%)
  blocking collectives  9.71 us (5%)
  starting transfers between devices  7.98 us (4%)
  other arithmetic  2.89 us (2%)
    ppermute x6, waiting for transfers between devices, exchange(): out.append(lax.ppermute(x, axis, perm))  114 us
    pallas_call x1, Pallas kernels, block_product(): pl.pallas_call(product_kernel, grid_spec=grid_spec, out_shape=jax.ShapeDt...  18.3 us
    all_gather x1, waiting for transfers between devices, local(): piece_blocks = lax.all_gather(right_blocks, 'col', axis=0, tiled=True)  9.89 us
    squeeze x1, blocking collectives, local(): targets = jnp.take(piece_cols[:, 0], panel_cols, axis=0) - row_rank * NJR  9.71 us
    ppermute x6, starting transfers between devices, exchange(): out.append(lax.ppermute(x, axis, perm))  7.98 us
  transfers between devices with their start and end apart: 7, of which 7 were waited for; matrix products, arithmetic and copies ran while one was open for 7% of the time, Pallas kernels for 0%

profile of v6, /device:TPU:0, one launch (start us, length us, event | category | flops | bytes accessed | tf_op | source)
XLA Modules:
  0.0 188.1 jit_solution(9581422173466546148)
XLA Ops:
  6.5 0.0 all-gather.2.cloned.1.call-start
  6.5 0.7 all-gather.2.cloned.1.call-update
  7.3 0.8 copy.63
  8.0 3.9 %collective-permute-start.2 = (s32[12,8]{1,0:T(8,128)S(1)}, s32[12,8]{1,0:T(8,128)S(1)}, u32[]{:S(2)}, u32[]{:S(2)}) collective-permute-start(s32[12,8]{1,0:T(8,128)S(1)} %copy.63), channel_id=1, source_target_pairs={{0,24},{8,16},{16,8},{24,0},{1,25},{9,17},{17,9},{25,1},{2,26},{10... | collective-permute-start | bytes 1160 | tf_op jit(solution)/shard_map/ppermute | solution.py:115
  11.9 0.5 collective-permute-start.1
  12.5 0.1 collective-permute-start
  12.5 1.1 collective-permute-done.2
  13.6 2.0 %collective-permute-done.1 = s32[12,8]{1,0:T(8,128)S(1)} collective-permute-done((s32[12,8]{1,0:T(8,128)S(1)}, s32[12,8]{1,0:T(8,128)S(1)}, u32[]{:S(2)}, u32[]{:S(2)}) %collective-permute-start.1) | collective-permute-done | bytes 416 | tf_op jit(solution)/shard_map/ppermute | solution.py:115
  15.6 0.5 collective-permute-done
  16.1 0.1 pad_add_fusion
  16.2 1.5 collective-permute-start.5
  17.7 0.1 collective-permute-start.4
  17.8 1.9 %collective-permute-start.3 = (bf16[12,8,128,128]{3,2,1,0:T(8,128)(2,1)}, bf16[12,8,128,128]{3,2,1,0:T(8,128)(2,1)}, u32[]{:S(2)}, u32[]{:S(2)}) collective-permute-start(bf16[12,8,128,128]{3,2,1,0:T(8,128)(2,1)} %refs_0_), channel_id=1, source_target_pairs={{0,8},{8,0},{16,24},{24,16},{1,9},{9,1},{17,25},{25,17},{2,10},{10... | collective-permute-start | bytes 9437192 | tf_op jit(solution)/shard_map/ppermute | solution.py:115
  19.7 0.7 broadcast_subtract_fusion
  20.4 0.1 copy.64
  20.5 1.2 dynamic-slice
  22.4 0.8 bitcast_dynamic-update-slice_fusion
  23.2 9.7 %all-reduce.1 = s32[512]{0:T(512)S(1)} all-reduce(s32[512]{0:T(512)S(1)} %bitcast_dynamic-update-slice_fusion), channel_id=1, replica_groups=mesh['row'=4,'col'=8] {'col'}, use_global_device_ids=true, to_apply=%add.1 | all-reduce | flops 512 | bytes 4096 | tf_op jit(solution)/shard_map/squeeze | solution.py:128
  32.9 0.1 stack.16
  33.0 0.1 reshape.90
  33.0 2.8 %gather_fusion = s32[384]{0:T(512)S(1)} fusion(s32[512]{0:T(512)S(1)} %all-reduce.1, s32[1024]{0:T(1024)S(1)} %pad_clamp_fusion), kind=kCustom, calls=%fused_computation | custom fusion | bytes 4608 | tf_op jit(solution)/shard_map/jit(_take)/gather | solution.py:128
  35.8 0.1 reshape.89
  35.9 0.1 compare_reduce_fusion
  36.0 0.1 fusion
  36.1 0.1 fusion.1
  36.2 0.1 stack_broadcast_in_dim.7
  36.3 0.1 stack_broadcast_in_dim.8
  36.4 0.1 copy.65
  36.5 0.1 reshape.86
  36.6 0.8 sort.34
  37.4 0.1 copy.67
  37.5 0.8 sort.35
  38.3 0.1 copy.66
  38.4 0.1 stack.17
  38.5 0.1 reshape.96
  38.5 2.9 %gather_fusion.1 = s32[384]{0:T(512)S(1)} fusion(s32[12,32]{1,0:T(8,128)S(1)} %get-tuple-element.14, s32[384]{0:T(512)S(1)} %reshape.96), kind=kCustom, calls=%fused_computation.1 | custom fusion | bytes 6144 | tf_op jit(solution)/shard_map/jit(take_along_axis)/gather | solution.py:132
  41.4 0.1 reshape.99
  41.5 0.1 select_n.48
  41.6 0.1 slice_compare_fusion
  41.7 0.1 pad_convert_fusion
  41.7 0.1 reshape.87
  41.8 0.6 stack.20.table_ref
  42.4 45.8 %collective-permute-done.5.refs_3_ = bf16[12,8,128,128]{3,2,1,0:T(8,128)(2,1)S(1)} collective-permute-done((bf16[12,8,128,128]{3,2,1,0:T(8,128)(2,1)}, bf16[12,8,128,128]{3,2,1,0:T(8,128)(2,1)S(1)}, u32[]{:S(2)}, u32[]{:S(2)}) %collective-permute-start.5) | collective-permute-done | bytes 3145760 | tf_op jit(solution)/shard_map/ppermute | solution.py:115
  88.3 0.0 copy-start
  88.3 64.7 %collective-permute-done.4.refs_2_ = bf16[12,8,128,128]{3,2,1,0:T(8,128)(2,1)} collective-permute-done((bf16[12,8,128,128]{3,2,1,0:T(8,128)(2,1)}, bf16[12,8,128,128]{3,2,1,0:T(8,128)(2,1)}, u32[]{:S(2)}, u32[]{:S(2)}) %collective-permute-start.4) | collective-permute-done | bytes 3145760 | tf_op jit(solution)/shard_map/ppermute | solution.py:115
  152.9 0.1 collective-permute-done.3.refs_1_
  153.1 9.9 %all-gather.2.cloned.1.call-done = bf16[512,1,128,128]{3,2,1,0:T(8,128)(2,1)} async-done(((bf16[64,1,128,128]{3,2,1,0:T(8,128)(2,1)}), bf16[512,1,128,128]{3,2,1,0:T(8,128)(2,1)}) %all-gather.2.cloned.1.call-update) | async-done | bytes 16777232 | tf_op jit(solution)/shard_map/all_gather | solution.py:123
  162.9 0.0 copy-done
  162.9 18.3 %shard_map.55 = bf16[12,4,128,128]{3,2,1,0:T(8,128)(2,1)} custom-call(s32[6,384]{1,0:T(8,128)} %stack.20.table_ref, bf16[12,8,128,128]{3,2,1,0:T(8,128)(2,1)} %refs_0_, bf16[12,8,128,128]{3,2,1,0:T(8,128)(2,1)} %collective-permute-done.3.refs_1_, bf16[12,8,128,128]{3,2,1,0:T(8,128)(2,1)} %collective-permute-done.4.refs_2_, ...), custom_call_target="tpu_custom_call" | custom-call | flops 1610612736 | bytes 26738688 | tf_op jit(solution)/shard_map/pallas_call | solution.py:102
  (9 shorter events, 0.1 us)
Async XLA Ops:
  6.5 156.4 %all-gather.2.cloned.1.call-start = ((), (), s32[]{:S(2)}) async-start(), calls=%async_computation | async-start | bytes 18874368 | tf_op jit(solution)/shard_map/all_gather | solution.py:123
  8.0 5.6 %collective-permute-start.2 = (s32[12,8]{1,0:T(8,128)S(1)}, s32[12,8]{1,0:T(8,128)S(1)}, u32[]{:S(2)}, u32[]{:S(2)}) collective-permute-start(s32[12,8]{1,0:T(8,128)S(1)} %copy.63), channel_id=1, source_target_pairs={{0,24},{8,16},{16,8},{24,0},{1,25},{9,17},{17,9},{25,1},{2,26},{10... | collective-permute-start | bytes 1160 | tf_op jit(solution)/shard_map/ppermute | solution.py:115
  11.9 3.7 %collective-permute-start.1 = (s32[12,8]{1,0:T(8,128)S(1)}, s32[12,8]{1,0:T(8,128)S(1)}, u32[]{:S(2)}, u32[]{:S(2)}) collective-permute-start(s32[12,8]{1,0:T(8,128)S(1)} %copy.63), channel_id=1, source_target_pairs={{0,16},{8,24},{16,0},{24,8},{1,17},{9,25},{17,1},{25,9},{2,18},{10... | collective-permute-start | bytes 1160 | tf_op jit(solution)/shard_map/ppermute | solution.py:115
  12.5 3.7 %collective-permute-start = (s32[12,8]{1,0:T(8,128)S(1)}, s32[12,8]{1,0:T(8,128)S(1)}, u32[]{:S(2)}, u32[]{:S(2)}) collective-permute-start(s32[12,8]{1,0:T(8,128)S(1)} %copy.63), channel_id=1, source_target_pairs={{0,8},{8,0},{16,24},{24,16},{1,9},{9,1},{17,25},{25,17},{2,10},{10... | collective-permute-start | bytes 1160 | tf_op jit(solution)/shard_map/ppermute | solution.py:115
  16.2 72.1 %collective-permute-start.5 = (bf16[12,8,128,128]{3,2,1,0:T(8,128)(2,1)}, bf16[12,8,128,128]{3,2,1,0:T(8,128)(2,1)S(1)}, u32[]{:S(2)}, u32[]{:S(2)}) collective-permute-start(bf16[12,8,128,128]{3,2,1,0:T(8,128)(2,1)} %refs_0_), channel_id=1, source_target_pairs={{0,24},{8,16},{16,8},{24,0},{1,25},{9,17},{17,9},{25,1},{2,26},{10... | collective-permute-start | bytes 9437192 | tf_op jit(solution)/shard_map/ppermute | solution.py:115
  17.7 135.3 %collective-permute-start.4 = (bf16[12,8,128,128]{3,2,1,0:T(8,128)(2,1)}, bf16[12,8,128,128]{3,2,1,0:T(8,128)(2,1)}, u32[]{:S(2)}, u32[]{:S(2)}) collective-permute-start(bf16[12,8,128,128]{3,2,1,0:T(8,128)(2,1)} %refs_0_), channel_id=1, source_target_pairs={{0,16},{8,24},{16,0},{24,8},{1,17},{9,25},{17,1},{25,9},{2,18},{10... | collective-permute-start | bytes 9437192 | tf_op jit(solution)/shard_map/ppermute | solution.py:115
  17.8 135.3 %collective-permute-start.3 = (bf16[12,8,128,128]{3,2,1,0:T(8,128)(2,1)}, bf16[12,8,128,128]{3,2,1,0:T(8,128)(2,1)}, u32[]{:S(2)}, u32[]{:S(2)}) collective-permute-start(bf16[12,8,128,128]{3,2,1,0:T(8,128)(2,1)} %refs_0_), channel_id=1, source_target_pairs={{0,8},{8,0},{16,24},{24,16},{1,9},{9,1},{17,25},{25,17},{2,10},{10... | collective-permute-start | bytes 9437192 | tf_op jit(solution)/shard_map/ppermute | solution.py:115
  88.3 74.7 %copy-start = (bf16[12,8,128,128]{3,2,1,0:T(8,128)(2,1)}, bf16[12,8,128,128]{3,2,1,0:T(8,128)(2,1)S(1)}, u32[]{:S(2)}) copy-start(bf16[12,8,128,128]{3,2,1,0:T(8,128)(2,1)S(1)} %collective-permute-done.5.refs_3_) | copy-start | bytes 9437188
Sparse Core Ops, SparseCore 0:
  8.9 153.9 all-gather.1

commit v7 on v5

--- a/solution.py
+++ b/solution.py
@@ -22,28 +22,30 @@
     pieces = refs[:n_pieces]
     right_hbm, out_ref, lbuf, rbuf, sem, acc_ref = refs[n_pieces:]
     i = pl.program_id(0)
-    rows = pl.num_programs(0)
+    steps = pl.num_programs(0)
     per_piece = pieces[0].shape[1]
     slots = n_pieces * per_piece
-    kr = out_ref.shape[0]
+    per_step, kr = out_ref.shape[0], out_ref.shape[1]
 
-    def left_copy(row, buf, s, pos):
+    def left_copy(row, buf, r, s, pos):
         return pltpu.make_async_copy(
-            pieces[s // per_piece].at[row, s % per_piece], lbuf.at[buf, pos], sem.at[0, buf, s]
+            pieces[s // per_piece].at[row, s % per_piece], lbuf.at[buf, r, pos], sem.at[0, buf, r, s]
         )
 
-    def right_copy(k, buf, s, pos):
-        return pltpu.make_async_copy(right_hbm.at[k], rbuf.at[buf, pos], sem.at[1, buf, s])
+    def right_copy(k, buf, r, s, pos):
+        return pltpu.make_async_copy(right_hbm.at[k], rbuf.at[buf, r, pos], sem.at[1, buf, r, s])
 
-    def fetch(row, buf):
-        for s in range(slots):
-            at = row * slots + s
+    def fetch(step, buf):
+        for r in range(per_step):
+            row = step * per_step + r
+            for s in range(slots):
+                at = row * slots + s
 
-            @pl.when(table_ref[2, at] != 0)
-            def _():
-                pos = table_ref[1, at]
-                left_copy(row, buf, s, pos).start()
-                right_copy(table_ref[0, at], buf, s, pos).start()
+                @pl.when(table_ref[2, at] != 0)
+                def _():
+                    pos = table_ref[1, at]
+                    left_copy(row, buf, r, s, pos).start()
+                    right_copy(table_ref[0, at], buf, r, s, pos).start()
 
     @pl.when(i == 0)
     def _():
@@ -51,40 +53,45 @@
 
     buf = i % 2
 
-    @pl.when(i + 1 < rows)
+    @pl.when(i + 1 < steps)
     def _():
         fetch(i + 1, 1 - buf)
 
-    for s in range(slots):
-        at = i * slots + s
+    for r in range(per_step):
+        row = i * per_step + r
+        for s in range(slots):
+            at = row * slots + s
 
-        @pl.when(table_ref[2, at] != 0)
-        def _():
-            left_copy(0, buf, s, s).wait()
-            right_copy(0, buf, s, s).wait()
+            @pl.when(table_ref[2, at] != 0)
+            def _():
+                left_copy(0, buf, r, s, s).wait()
+                right_copy(0, buf, r, s, s).wait()
 
-    acc_ref[...] = jnp.zeros_like(acc_ref)
-    acc = None
-    for j in range(slots):
-        at = i * slots + j
-        term = jnp.dot(lbuf[buf, j], rbuf[buf, j], preferred_element_type=jnp.float32)
-        acc = term if j == 0 else jnp.where(table_ref[4, at] != 0, term, acc + term)
-        acc_ref[table_ref[3, at]] = acc
-    out_ref[...] = acc_ref[0:kr].astype(out_ref.dtype)
+    for r in range(per_step):
+        row = i * per_step + r
+        acc_ref[...] = jnp.zeros_like(acc_ref)
+        acc = None
+        for j in range(slots):
+            at = row * slots + j
+            term = jnp.dot(lbuf[buf, r, j], rbuf[buf, r, j], preferred_element_type=jnp.float32)
+            acc = term if j == 0 else jnp.where(table_ref[4, at] != 0, term, acc + term)
+            acc_ref[table_ref[3, at]] = acc
+        out_ref[r] = acc_ref[0:kr].astype(out_ref.dtype)
 
 
 def block_product(table, pieces, right_flat, kr):
     rows, per_piece, bs, _ = pieces[0].shape
     slots = per_piece * len(pieces)
+    per_step = 2 if rows % 2 == 0 else 1
     grid_spec = pltpu.PrefetchScalarGridSpec(
         num_scalar_prefetch=1,
-        grid=(rows,),
+        grid=(rows // per_step,),
         in_specs=[pl.BlockSpec(memory_space=pl.ANY)] * (len(pieces) + 1),
-        out_specs=pl.BlockSpec((None, kr, bs, bs), lambda i, table: (i, 0, 0, 0)),
+        out_specs=pl.BlockSpec((per_step, kr, bs, bs), lambda i, table: (i, 0, 0, 0)),
         scratch_shapes=[
-            pltpu.VMEM((2, slots, bs, bs), pieces[0].dtype),
-            pltpu.VMEM((2, slots, bs, bs), right_flat.dtype),
-            pltpu.SemaphoreType.DMA((2, 2, slots)),
+            pltpu.VMEM((2, per_step, slots, bs, bs), pieces[0].dtype),
+            pltpu.VMEM((2, per_step, slots, bs, bs), right_flat.dtype),
+            pltpu.SemaphoreType.DMA((2, 2, per_step, slots)),
             pltpu.VMEM((kr + 1, bs, bs), jnp.float32),
         ],
     )

time: 186 us -> 185 us (level)
  no operation moved by 1% of the time
where the time goes in v7:
time: 185 us
  waiting for transfers between devices  125 us (68%)
  Pallas kernels  15.1 us (8%)
  between operations  14.1 us (8%)
  local copies, waits for them, and re-layouts  10.1 us (5%)
  blocking collectives  9.71 us (5%)
  starting transfers between devices  7.98 us (4%)
  other arithmetic  2.77 us (1%)
    ppermute x6, waiting for transfers between devices, exchange(): out.append(lax.ppermute(x, axis, perm))  114 us
    pallas_call x1, Pallas kernels, block_product(): pl.pallas_call(product_kernel, grid_spec=grid_spec, out_shape=jax.ShapeDt...  15.1 us
    all_gather x1, waiting for transfers between devices, local(): piece_blocks = lax.all_gather(right_blocks, 'col', axis=0, tiled=True)  9.89 us
    squeeze x1, blocking collectives, local(): targets = jnp.take(piece_cols[:, 0], panel_cols, axis=0) - row_rank * NJR  9.71 us
    ppermute x6, starting transfers between devices, exchange(): out.append(lax.ppermute(x, axis, perm))  7.98 us
  transfers between devices with their start and end apart: 7, of which 7 were waited for; matrix products, arithmetic and copies ran while one was open for 7% of the time, Pallas kernels for 0%

profile of v7, /device:TPU:0, one launch (start us, length us, event | category | flops | bytes accessed | tf_op | source)
XLA Modules:
  0.0 184.9 jit_solution(3818185180754692540)
XLA Ops:
  6.5 0.0 all-gather.2.cloned.1.call-start
  6.5 0.7 all-gather.2.cloned.1.call-update
  7.3 0.8 copy.63
  8.0 3.9 %collective-permute-start.2 = (s32[12,8]{1,0:T(8,128)S(1)}, s32[12,8]{1,0:T(8,128)S(1)}, u32[]{:S(2)}, u32[]{:S(2)}) collective-permute-start(s32[12,8]{1,0:T(8,128)S(1)} %copy.63), channel_id=1, source_target_pairs={{0,24},{8,16},{16,8},{24,0},{1,25},{9,17},{17,9},{25,1},{2,26},{10... | collective-permute-start | bytes 1160 | tf_op jit(solution)/shard_map/ppermute | solution.py:113
  11.9 0.5 collective-permute-start.1
  12.5 0.1 collective-permute-start
  12.5 1.1 collective-permute-done.2
  13.6 2.0 %collective-permute-done.1 = s32[12,8]{1,0:T(8,128)S(1)} collective-permute-done((s32[12,8]{1,0:T(8,128)S(1)}, s32[12,8]{1,0:T(8,128)S(1)}, u32[]{:S(2)}, u32[]{:S(2)}) %collective-permute-start.1) | collective-permute-done | bytes 416 | tf_op jit(solution)/shard_map/ppermute | solution.py:113
  15.6 0.5 collective-permute-done
  16.1 0.1 pad_add_fusion
  16.2 1.5 collective-permute-start.5
  17.7 0.1 collective-permute-start.4
  17.8 1.9 %collective-permute-start.3 = (bf16[12,8,128,128]{3,2,1,0:T(8,128)(2,1)}, bf16[12,8,128,128]{3,2,1,0:T(8,128)(2,1)}, u32[]{:S(2)}, u32[]{:S(2)}) collective-permute-start(bf16[12,8,128,128]{3,2,1,0:T(8,128)(2,1)} %refs_0_), channel_id=1, source_target_pairs={{0,8},{8,0},{16,24},{24,16},{1,9},{9,1},{17,25},{25,17},{2,10},{10... | collective-permute-start | bytes 9437192 | tf_op jit(solution)/shard_map/ppermute | solution.py:113
  19.7 0.7 broadcast_subtract_fusion
  20.4 0.1 copy.64
  20.5 1.2 dynamic-slice
  22.4 0.8 bitcast_dynamic-update-slice_fusion
  23.2 9.7 %all-reduce.1 = s32[512]{0:T(512)S(1)} all-reduce(s32[512]{0:T(512)S(1)} %bitcast_dynamic-update-slice_fusion), channel_id=1, replica_groups=mesh['row'=4,'col'=8] {'col'}, use_global_device_ids=true, to_apply=%add.1 | all-reduce | flops 512 | bytes 4096 | tf_op jit(solution)/shard_map/squeeze | solution.py:126
  32.9 0.1 stack.16
  33.0 0.1 reshape.86
  33.0 2.8 %gather_fusion = s32[384]{0:T(512)S(1)} fusion(s32[512]{0:T(512)S(1)} %all-reduce.1, s32[1024]{0:T(1024)S(1)} %pad_clamp_fusion), kind=kCustom, calls=%fused_computation | custom fusion | bytes 4608 | tf_op jit(solution)/shard_map/jit(_take)/gather | solution.py:126
  35.8 0.1 reshape.85
  35.9 0.1 compare_reduce_fusion
  36.0 0.1 fusion
  36.1 0.1 reshape.82
  36.2 0.1 copy.65
  36.3 0.8 sort.34
  37.1 0.1 copy.67
  37.2 0.8 sort.35
  38.0 0.1 copy.66
  38.1 0.1 stack.17
  38.2 0.1 reshape.92
  38.3 2.9 %gather_fusion.1 = s32[384]{0:T(512)S(1)} fusion(s32[12,32]{1,0:T(8,128)S(1)} %get-tuple-element.14, s32[384]{0:T(512)S(1)} %reshape.92), kind=kCustom, calls=%fused_computation.1 | custom fusion | bytes 6144 | tf_op jit(solution)/shard_map/jit(take_along_axis)/gather | solution.py:130
  41.1 0.1 reshape.95
  41.2 0.1 select_n.48
  41.3 0.1 slice_compare_fusion
  41.4 0.1 pad_convert_fusion
  41.5 0.1 reshape.83
  41.5 0.6 stack.20.table_ref
  42.2 46.1 %collective-permute-done.5.refs_3_ = bf16[12,8,128,128]{3,2,1,0:T(8,128)(2,1)S(1)} collective-permute-done((bf16[12,8,128,128]{3,2,1,0:T(8,128)(2,1)}, bf16[12,8,128,128]{3,2,1,0:T(8,128)(2,1)S(1)}, u32[]{:S(2)}, u32[]{:S(2)}) %collective-permute-start.5) | collective-permute-done | bytes 3145760 | tf_op jit(solution)/shard_map/ppermute | solution.py:113
  88.3 0.0 copy-start
  88.3 64.7 %collective-permute-done.4.refs_2_ = bf16[12,8,128,128]{3,2,1,0:T(8,128)(2,1)} collective-permute-done((bf16[12,8,128,128]{3,2,1,0:T(8,128)(2,1)}, bf16[12,8,128,128]{3,2,1,0:T(8,128)(2,1)}, u32[]{:S(2)}, u32[]{:S(2)}) %collective-permute-start.4) | collective-permute-done | bytes 3145760 | tf_op jit(solution)/shard_map/ppermute | solution.py:113
  152.9 0.1 collective-permute-done.3.refs_1_
  153.1 9.9 %all-gather.2.cloned.1.call-done = bf16[512,1,128,128]{3,2,1,0:T(8,128)(2,1)} async-done(((bf16[64,1,128,128]{3,2,1,0:T(8,128)(2,1)}), bf16[512,1,128,128]{3,2,1,0:T(8,128)(2,1)}) %all-gather.2.cloned.1.call-update) | async-done | bytes 16777232 | tf_op jit(solution)/shard_map/all_gather | solution.py:121
  162.9 0.0 copy-done
  162.9 15.1 %shard_map.55 = bf16[12,4,128,128]{3,2,1,0:T(8,128)(2,1)} custom-call(s32[5,384]{1,0:T(8,128)} %stack.20.table_ref, bf16[12,8,128,128]{3,2,1,0:T(8,128)(2,1)} %refs_0_, bf16[12,8,128,128]{3,2,1,0:T(8,128)(2,1)} %collective-permute-done.3.refs_1_, bf16[12,8,128,128]{3,2,1,0:T(8,128)(2,1)} %collective-permute-done.4.refs_2_, ...), custom_call_target="tpu_custom_call" | custom-call | flops 1610612736 | bytes 26738688 | tf_op jit(solution)/shard_map/pallas_call | solution.py:100
  (9 shorter events, 0.1 us)
Async XLA Ops:
  6.5 156.4 %all-gather.2.cloned.1.call-start = ((), (), s32[]{:S(2)}) async-start(), calls=%async_computation | async-start | bytes 18874368 | tf_op jit(solution)/shard_map/all_gather | solution.py:121
  8.0 5.6 %collective-permute-start.2 = (s32[12,8]{1,0:T(8,128)S(1)}, s32[12,8]{1,0:T(8,128)S(1)}, u32[]{:S(2)}, u32[]{:S(2)}) collective-permute-start(s32[12,8]{1,0:T(8,128)S(1)} %copy.63), channel_id=1, source_target_pairs={{0,24},{8,16},{16,8},{24,0},{1,25},{9,17},{17,9},{25,1},{2,26},{10... | collective-permute-start | bytes 1160 | tf_op jit(solution)/shard_map/ppermute | solution.py:113
  11.9 3.7 %collective-permute-start.1 = (s32[12,8]{1,0:T(8,128)S(1)}, s32[12,8]{1,0:T(8,128)S(1)}, u32[]{:S(2)}, u32[]{:S(2)}) collective-permute-start(s32[12,8]{1,0:T(8,128)S(1)} %copy.63), channel_id=1, source_target_pairs={{0,16},{8,24},{16,0},{24,8},{1,17},{9,25},{17,1},{25,9},{2,18},{10... | collective-permute-start | bytes 1160 | tf_op jit(solution)/shard_map/ppermute | solution.py:113
  12.5 3.7 %collective-permute-start = (s32[12,8]{1,0:T(8,128)S(1)}, s32[12,8]{1,0:T(8,128)S(1)}, u32[]{:S(2)}, u32[]{:S(2)}) collective-permute-start(s32[12,8]{1,0:T(8,128)S(1)} %copy.63), channel_id=1, source_target_pairs={{0,8},{8,0},{16,24},{24,16},{1,9},{9,1},{17,25},{25,17},{2,10},{10... | collective-permute-start | bytes 1160 | tf_op jit(solution)/shard_map/ppermute | solution.py:113
  16.2 72.1 %collective-permute-start.5 = (bf16[12,8,128,128]{3,2,1,0:T(8,128)(2,1)}, bf16[12,8,128,128]{3,2,1,0:T(8,128)(2,1)S(1)}, u32[]{:S(2)}, u32[]{:S(2)}) collective-permute-start(bf16[12,8,128,128]{3,2,1,0:T(8,128)(2,1)} %refs_0_), channel_id=1, source_target_pairs={{0,24},{8,16},{16,8},{24,0},{1,25},{9,17},{17,9},{25,1},{2,26},{10... | collective-permute-start | bytes 9437192 | tf_op jit(solution)/shard_map/ppermute | solution.py:113
  17.7 135.3 %collective-permute-start.4 = (bf16[12,8,128,128]{3,2,1,0:T(8,128)(2,1)}, bf16[12,8,128,128]{3,2,1,0:T(8,128)(2,1)}, u32[]{:S(2)}, u32[]{:S(2)}) collective-permute-start(bf16[12,8,128,128]{3,2,1,0:T(8,128)(2,1)} %refs_0_), channel_id=1, source_target_pairs={{0,16},{8,24},{16,0},{24,8},{1,17},{9,25},{17,1},{25,9},{2,18},{10... | collective-permute-start | bytes 9437192 | tf_op jit(solution)/shard_map/ppermute | solution.py:113
  17.8 135.3 %collective-permute-start.3 = (bf16[12,8,128,128]{3,2,1,0:T(8,128)(2,1)}, bf16[12,8,128,128]{3,2,1,0:T(8,128)(2,1)}, u32[]{:S(2)}, u32[]{:S(2)}) collective-permute-start(bf16[12,8,128,128]{3,2,1,0:T(8,128)(2,1)} %refs_0_), channel_id=1, source_target_pairs={{0,8},{8,0},{16,24},{24,16},{1,9},{9,1},{17,25},{25,17},{2,10},{10... | collective-permute-start | bytes 9437192 | tf_op jit(solution)/shard_map/ppermute | solution.py:113
  88.3 74.7 %copy-start = (bf16[12,8,128,128]{3,2,1,0:T(8,128)(2,1)}, bf16[12,8,128,128]{3,2,1,0:T(8,128)(2,1)S(1)}, u32[]{:S(2)}) copy-start(bf16[12,8,128,128]{3,2,1,0:T(8,128)(2,1)S(1)} %collective-permute-done.5.refs_3_) | copy-start | bytes 9437188
Sparse Core Ops, SparseCore 0:
  8.9 153.9 all-gather.1

commit v8 on v7

--- a/solution.py
+++ b/solution.py
@@ -27,9 +27,9 @@
     slots = n_pieces * per_piece
     per_step, kr = out_ref.shape[0], out_ref.shape[1]
 
-    def left_copy(row, buf, r, s, pos):
+    def left_copy(row, buf, r, p):
         return pltpu.make_async_copy(
-            pieces[s // per_piece].at[row, s % per_piece], lbuf.at[buf, r, pos], sem.at[0, buf, r, s]
+            pieces[p].at[row], lbuf.at[buf, r, pl.ds(p * per_piece, per_piece)], sem.at[0, buf, r, p]
         )
 
     def right_copy(k, buf, r, s, pos):
@@ -38,14 +38,14 @@
     def fetch(step, buf):
         for r in range(per_step):
             row = step * per_step + r
+            for p in range(n_pieces):
+                left_copy(row, buf, r, p).start()
             for s in range(slots):
                 at = row * slots + s
 
                 @pl.when(table_ref[2, at] != 0)
                 def _():
-                    pos = table_ref[1, at]
-                    left_copy(row, buf, r, s, pos).start()
-                    right_copy(table_ref[0, at], buf, r, s, pos).start()
+                    right_copy(table_ref[0, at], buf, r, s, table_ref[1, at]).start()
 
     @pl.when(i == 0)
     def _():
@@ -59,12 +59,13 @@
 
     for r in range(per_step):
         row = i * per_step + r
+        for p in range(n_pieces):
+            left_copy(0, buf, r, p).wait()
         for s in range(slots):
             at = row * slots + s
 
             @pl.when(table_ref[2, at] != 0)
             def _():
-                left_copy(0, buf, r, s, s).wait()
                 right_copy(0, buf, r, s, s).wait()
 
     for r in range(per_step):
@@ -73,7 +74,9 @@
         acc = None
         for j in range(slots):
             at = row * slots + j
-            term = jnp.dot(lbuf[buf, r, j], rbuf[buf, r, j], preferred_element_type=jnp.float32)
+            term = jnp.dot(
+                lbuf[buf, r, table_ref[5, at]], rbuf[buf, r, j], preferred_element_type=jnp.float32
+            )
             acc = term if j == 0 else jnp.where(table_ref[4, at] != 0, term, acc + term)
             acc_ref[table_ref[3, at]] = acc
         out_ref[r] = acc_ref[0:kr].astype(out_ref.dtype)
@@ -134,7 +137,7 @@
     )
     position = jnp.argsort(order, axis=1).astype(jnp.int32)
     used = (slot < keep_cols.shape[1]).astype(jnp.int32)
-    table = jnp.stack([panel_cols, position, used, sorted_slot, start]).reshape(5, rows * slots)
+    table = jnp.stack([panel_cols, position, used, sorted_slot, start, order]).reshape(6, rows * slots)
     return block_product(table, pieces, piece_blocks[:, 0], keep_cols.shape[1])
 
 

time: 185 us -> 186 us (level)
  no operation moved by 1% of the time
where the time goes in v8:
time: 186 us; the launch traced here: 185 us
  waiting for transfers between devices  125 us (67%)
  Pallas kernels  15.6 us (8%)
  between operations  14.1 us (8%)
  local copies, waits for them, and re-layouts  10.2 us (5%)
  blocking collectives  9.71 us (5%)
  starting transfers between devices  7.98 us (4%)
  other arithmetic  2.77 us (1%)
    ppermute x6, waiting for transfers between devices, exchange(): out.append(lax.ppermute(x, axis, perm))  114 us
    pallas_call x1, Pallas kernels, block_product(): pl.pallas_call(product_kernel, grid_spec=grid_spec, out_shape=jax.ShapeDt...  15.6 us
    all_gather x1, waiting for transfers between devices, local(): piece_blocks = lax.all_gather(right_blocks, 'col', axis=0, tiled=True)  9.89 us
    squeeze x1, blocking collectives, local(): targets = jnp.take(piece_cols[:, 0], panel_cols, axis=0) - row_rank * NJR  9.71 us
    ppermute x6, starting transfers between devices, exchange(): out.append(lax.ppermute(x, axis, perm))  7.98 us
  transfers between devices with their start and end apart: 7, of which 7 were waited for; matrix products, arithmetic and copies ran while one was open for 7% of the time, Pallas kernels for 0%

profile of v8, /device:TPU:0, one launch (start us, length us, event | category | flops | bytes accessed | tf_op | source)
XLA Modules:
  0.0 185.4 jit_solution(16500651304916127641)
XLA Ops:
  6.5 0.0 all-gather.2.cloned.1.call-start
  6.5 0.7 all-gather.2.cloned.1.call-update
  7.3 0.8 copy.68
  8.0 3.9 %collective-permute-start.2 = (s32[12,8]{1,0:T(8,128)S(1)}, s32[12,8]{1,0:T(8,128)S(1)}, u32[]{:S(2)}, u32[]{:S(2)}) collective-permute-start(s32[12,8]{1,0:T(8,128)S(1)} %copy.68), channel_id=1, source_target_pairs={{0,24},{8,16},{16,8},{24,0},{1,25},{9,17},{17,9},{25,1},{2,26},{10... | collective-permute-start | bytes 1160 | tf_op jit(solution)/shard_map/ppermute | solution.py:116
  11.9 0.5 collective-permute-start.1
  12.5 0.1 collective-permute-start
  12.5 1.1 collective-permute-done.2
  13.6 2.0 %collective-permute-done.1 = s32[12,8]{1,0:T(8,128)S(1)} collective-permute-done((s32[12,8]{1,0:T(8,128)S(1)}, s32[12,8]{1,0:T(8,128)S(1)}, u32[]{:S(2)}, u32[]{:S(2)}) %collective-permute-start.1) | collective-permute-done | bytes 416 | tf_op jit(solution)/shard_map/ppermute | solution.py:116
  15.6 0.5 collective-permute-done
  16.1 0.1 pad_add_fusion
  16.2 1.5 collective-permute-start.5
  17.7 0.1 collective-permute-start.4
  17.8 1.9 %collective-permute-start.3 = (bf16[12,8,128,128]{3,2,1,0:T(8,128)(2,1)}, bf16[12,8,128,128]{3,2,1,0:T(8,128)(2,1)}, u32[]{:S(2)}, u32[]{:S(2)}) collective-permute-start(bf16[12,8,128,128]{3,2,1,0:T(8,128)(2,1)} %refs_0_), channel_id=1, source_target_pairs={{0,8},{8,0},{16,24},{24,16},{1,9},{9,1},{17,25},{25,17},{2,10},{10... | collective-permute-start | bytes 9437192 | tf_op jit(solution)/shard_map/ppermute | solution.py:116
  19.7 0.7 broadcast_subtract_fusion
  20.4 0.1 copy.69
  20.5 1.2 dynamic-slice
  22.4 0.8 bitcast_dynamic-update-slice_fusion
  23.2 9.7 %all-reduce.1 = s32[512]{0:T(512)S(1)} all-reduce(s32[512]{0:T(512)S(1)} %bitcast_dynamic-update-slice_fusion), channel_id=1, replica_groups=mesh['row'=4,'col'=8] {'col'}, use_global_device_ids=true, to_apply=%add.1 | all-reduce | flops 512 | bytes 4096 | tf_op jit(solution)/shard_map/squeeze | solution.py:129
  32.9 0.1 stack.19
  33.0 0.1 reshape.88
  33.0 2.8 %gather_fusion = s32[384]{0:T(512)S(1)} fusion(s32[512]{0:T(512)S(1)} %all-reduce.1, s32[1024]{0:T(1024)S(1)} %pad_clamp_fusion), kind=kCustom, calls=%fused_computation | custom fusion | bytes 4608 | tf_op jit(solution)/shard_map/jit(_take)/gather | solution.py:129
  35.8 0.1 reshape.87
  35.9 0.1 compare_reduce_fusion
  36.0 0.1 fusion
  36.1 0.1 reshape.84
  36.2 0.1 copy.70
  36.3 0.8 sort.34
  37.1 0.1 copy.72
  37.2 0.8 sort.35
  38.0 0.1 copy.71
  38.1 0.1 stack.20
  38.2 0.1 stack.23
  38.3 0.1 reshape.94
  38.3 2.9 %gather_fusion.1 = s32[384]{0:T(512)S(1)} fusion(s32[12,32]{1,0:T(8,128)S(1)} %get-tuple-element.14, s32[384]{0:T(512)S(1)} %reshape.94), kind=kCustom, calls=%fused_computation.1 | custom fusion | bytes 6144 | tf_op jit(solution)/shard_map/jit(take_along_axis)/gather | solution.py:133
  41.2 0.1 reshape.97
  41.3 0.1 select_n.48
  41.4 0.1 slice_compare_fusion
  41.5 0.1 pad_convert_fusion
  41.5 0.1 reshape.85
  41.6 0.6 stack.24.table_ref
  42.2 46.0 %collective-permute-done.5.refs_3_ = bf16[12,8,128,128]{3,2,1,0:T(8,128)(2,1)S(1)} collective-permute-done((bf16[12,8,128,128]{3,2,1,0:T(8,128)(2,1)}, bf16[12,8,128,128]{3,2,1,0:T(8,128)(2,1)S(1)}, u32[]{:S(2)}, u32[]{:S(2)}) %collective-permute-start.5) | collective-permute-done | bytes 3145760 | tf_op jit(solution)/shard_map/ppermute | solution.py:116
  88.3 0.0 copy-start
  88.3 64.7 %collective-permute-done.4.refs_2_ = bf16[12,8,128,128]{3,2,1,0:T(8,128)(2,1)} collective-permute-done((bf16[12,8,128,128]{3,2,1,0:T(8,128)(2,1)}, bf16[12,8,128,128]{3,2,1,0:T(8,128)(2,1)}, u32[]{:S(2)}, u32[]{:S(2)}) %collective-permute-start.4) | collective-permute-done | bytes 3145760 | tf_op jit(solution)/shard_map/ppermute | solution.py:116
  152.9 0.1 collective-permute-done.3.refs_1_
  153.1 9.9 %all-gather.2.cloned.1.call-done = bf16[512,1,128,128]{3,2,1,0:T(8,128)(2,1)} async-done(((bf16[64,1,128,128]{3,2,1,0:T(8,128)(2,1)}), bf16[512,1,128,128]{3,2,1,0:T(8,128)(2,1)}) %all-gather.2.cloned.1.call-update) | async-done | bytes 16777232 | tf_op jit(solution)/shard_map/all_gather | solution.py:124
  162.9 0.0 copy-done
  162.9 15.6 %shard_map.55 = bf16[12,4,128,128]{3,2,1,0:T(8,128)(2,1)} custom-call(s32[6,384]{1,0:T(8,128)} %stack.24.table_ref, bf16[12,8,128,128]{3,2,1,0:T(8,128)(2,1)} %refs_0_, bf16[12,8,128,128]{3,2,1,0:T(8,128)(2,1)} %collective-permute-done.3.refs_1_, bf16[12,8,128,128]{3,2,1,0:T(8,128)(2,1)} %collective-permute-done.4.refs_2_, ...), custom_call_target="tpu_custom_call" | custom-call | flops 1610612736 | bytes 26738688 | tf_op jit(solution)/shard_map/pallas_call | solution.py:103
  (9 shorter events, 0.1 us)
Async XLA Ops:
  6.5 156.4 %all-gather.2.cloned.1.call-start = ((), (), s32[]{:S(2)}) async-start(), calls=%async_computation | async-start | bytes 18874368 | tf_op jit(solution)/shard_map/all_gather | solution.py:124
  8.0 5.6 %collective-permute-start.2 = (s32[12,8]{1,0:T(8,128)S(1)}, s32[12,8]{1,0:T(8,128)S(1)}, u32[]{:S(2)}, u32[]{:S(2)}) collective-permute-start(s32[12,8]{1,0:T(8,128)S(1)} %copy.68), channel_id=1, source_target_pairs={{0,24},{8,16},{16,8},{24,0},{1,25},{9,17},{17,9},{25,1},{2,26},{10... | collective-permute-start | bytes 1160 | tf_op jit(solution)/shard_map/ppermute | solution.py:116
  11.9 3.7 %collective-permute-start.1 = (s32[12,8]{1,0:T(8,128)S(1)}, s32[12,8]{1,0:T(8,128)S(1)}, u32[]{:S(2)}, u32[]{:S(2)}) collective-permute-start(s32[12,8]{1,0:T(8,128)S(1)} %copy.68), channel_id=1, source_target_pairs={{0,16},{8,24},{16,0},{24,8},{1,17},{9,25},{17,1},{25,9},{2,18},{10... | collective-permute-start | bytes 1160 | tf_op jit(solution)/shard_map/ppermute | solution.py:116
  12.5 3.7 %collective-permute-start = (s32[12,8]{1,0:T(8,128)S(1)}, s32[12,8]{1,0:T(8,128)S(1)}, u32[]{:S(2)}, u32[]{:S(2)}) collective-permute-start(s32[12,8]{1,0:T(8,128)S(1)} %copy.68), channel_id=1, source_target_pairs={{0,8},{8,0},{16,24},{24,16},{1,9},{9,1},{17,25},{25,17},{2,10},{10... | collective-permute-start | bytes 1160 | tf_op jit(solution)/shard_map/ppermute | solution.py:116
  16.2 72.1 %collective-permute-start.5 = (bf16[12,8,128,128]{3,2,1,0:T(8,128)(2,1)}, bf16[12,8,128,128]{3,2,1,0:T(8,128)(2,1)S(1)}, u32[]{:S(2)}, u32[]{:S(2)}) collective-permute-start(bf16[12,8,128,128]{3,2,1,0:T(8,128)(2,1)} %refs_0_), channel_id=1, source_target_pairs={{0,24},{8,16},{16,8},{24,0},{1,25},{9,17},{17,9},{25,1},{2,26},{10... | collective-permute-start | bytes 9437192 | tf_op jit(solution)/shard_map/ppermute | solution.py:116
  17.7 135.3 %collective-permute-start.4 = (bf16[12,8,128,128]{3,2,1,0:T(8,128)(2,1)}, bf16[12,8,128,128]{3,2,1,0:T(8,128)(2,1)}, u32[]{:S(2)}, u32[]{:S(2)}) collective-permute-start(bf16[12,8,128,128]{3,2,1,0:T(8,128)(2,1)} %refs_0_), channel_id=1, source_target_pairs={{0,16},{8,24},{16,0},{24,8},{1,17},{9,25},{17,1},{25,9},{2,18},{10... | collective-permute-start | bytes 9437192 | tf_op jit(solution)/shard_map/ppermute | solution.py:116
  17.8 135.3 %collective-permute-start.3 = (bf16[12,8,128,128]{3,2,1,0:T(8,128)(2,1)}, bf16[12,8,128,128]{3,2,1,0:T(8,128)(2,1)}, u32[]{:S(2)}, u32[]{:S(2)}) collective-permute-start(bf16[12,8,128,128]{3,2,1,0:T(8,128)(2,1)} %refs_0_), channel_id=1, source_target_pairs={{0,8},{8,0},{16,24},{24,16},{1,9},{9,1},{17,25},{25,17},{2,10},{10... | collective-permute-start | bytes 9437192 | tf_op jit(solution)/shard_map/ppermute | solution.py:116
  88.3 74.7 %copy-start = (bf16[12,8,128,128]{3,2,1,0:T(8,128)(2,1)}, bf16[12,8,128,128]{3,2,1,0:T(8,128)(2,1)S(1)}, u32[]{:S(2)}) copy-start(bf16[12,8,128,128]{3,2,1,0:T(8,128)(2,1)S(1)} %collective-permute-done.5.refs_3_) | copy-start | bytes 9437188
Sparse Core Ops, SparseCore 0:
  8.9 153.9 all-gather.1

commit v9 on v7

--- a/solution.py
+++ b/solution.py
@@ -82,7 +82,7 @@
 def block_product(table, pieces, right_flat, kr):
     rows, per_piece, bs, _ = pieces[0].shape
     slots = per_piece * len(pieces)
-    per_step = 2 if rows % 2 == 0 else 1
+    per_step = 3 if rows % 3 == 0 else 1
     grid_spec = pltpu.PrefetchScalarGridSpec(
         num_scalar_prefetch=1,
         grid=(rows // per_step,),

time: 185 us -> 186 us (level)
  no operation moved by 1% of the time
where the time goes in v9:
time: 186 us
  waiting for transfers between devices  125 us (67%)
  Pallas kernels  16.4 us (9%)
  between operations  14.1 us (8%)
  local copies, waits for them, and re-layouts  10.1 us (5%)
  blocking collectives  9.71 us (5%)
  starting transfers between devices  7.98 us (4%)
  other arithmetic  2.77 us (1%)
    ppermute x6, waiting for transfers between devices, exchange(): out.append(lax.ppermute(x, axis, perm))  114 us
    pallas_call x1, Pallas kernels, block_product(): pl.pallas_call(product_kernel, grid_spec=grid_spec, out_shape=jax.ShapeDt...  16.4 us
    all_gather x1, waiting for transfers between devices, local(): piece_blocks = lax.all_gather(right_blocks, 'col', axis=0, tiled=True)  9.89 us
    squeeze x1, blocking collectives, local(): targets = jnp.take(piece_cols[:, 0], panel_cols, axis=0) - row_rank * NJR  9.71 us
    ppermute x6, starting transfers between devices, exchange(): out.append(lax.ppermute(x, axis, perm))  7.98 us
  transfers between devices with their start and end apart: 7, of which 7 were waited for; matrix products, arithmetic and copies ran while one was open for 7% of the time, Pallas kernels for 0%

profile of v9, /device:TPU:0, one launch (start us, length us, event | category | flops | bytes accessed | tf_op | source)
XLA Modules:
  0.0 186.2 jit_solution(2860503224144161787)
XLA Ops:
  6.5 0.0 all-gather.2.cloned.1.call-start
  6.5 0.7 all-gather.2.cloned.1.call-update
  7.3 0.8 copy.63
  8.0 3.9 %collective-permute-start.2 = (s32[12,8]{1,0:T(8,128)S(1)}, s32[12,8]{1,0:T(8,128)S(1)}, u32[]{:S(2)}, u32[]{:S(2)}) collective-permute-start(s32[12,8]{1,0:T(8,128)S(1)} %copy.63), channel_id=1, source_target_pairs={{0,24},{8,16},{16,8},{24,0},{1,25},{9,17},{17,9},{25,1},{2,26},{10... | collective-permute-start | bytes 1160 | tf_op jit(solution)/shard_map/ppermute | solution.py:113
  11.9 0.5 collective-permute-start.1
  12.5 0.1 collective-permute-start
  12.5 1.1 collective-permute-done.2
  13.6 2.0 %collective-permute-done.1 = s32[12,8]{1,0:T(8,128)S(1)} collective-permute-done((s32[12,8]{1,0:T(8,128)S(1)}, s32[12,8]{1,0:T(8,128)S(1)}, u32[]{:S(2)}, u32[]{:S(2)}) %collective-permute-start.1) | collective-permute-done | bytes 416 | tf_op jit(solution)/shard_map/ppermute | solution.py:113
  15.6 0.5 collective-permute-done
  16.1 0.1 pad_add_fusion
  16.2 1.5 collective-permute-start.5
  17.7 0.1 collective-permute-start.4
  17.8 1.9 %collective-permute-start.3 = (bf16[12,8,128,128]{3,2,1,0:T(8,128)(2,1)}, bf16[12,8,128,128]{3,2,1,0:T(8,128)(2,1)}, u32[]{:S(2)}, u32[]{:S(2)}) collective-permute-start(bf16[12,8,128,128]{3,2,1,0:T(8,128)(2,1)} %refs_0_), channel_id=1, source_target_pairs={{0,8},{8,0},{16,24},{24,16},{1,9},{9,1},{17,25},{25,17},{2,10},{10... | collective-permute-start | bytes 9437192 | tf_op jit(solution)/shard_map/ppermute | solution.py:113
  19.7 0.7 broadcast_subtract_fusion
  20.4 0.1 copy.64
  20.5 1.2 dynamic-slice
  22.4 0.8 bitcast_dynamic-update-slice_fusion
  23.2 9.7 %all-reduce.1 = s32[512]{0:T(512)S(1)} all-reduce(s32[512]{0:T(512)S(1)} %bitcast_dynamic-update-slice_fusion), channel_id=1, replica_groups=mesh['row'=4,'col'=8] {'col'}, use_global_device_ids=true, to_apply=%add.1 | all-reduce | flops 512 | bytes 4096 | tf_op jit(solution)/shard_map/squeeze | solution.py:126
  32.9 0.1 stack.16
  33.0 0.1 reshape.86
  33.0 2.8 %gather_fusion = s32[384]{0:T(512)S(1)} fusion(s32[512]{0:T(512)S(1)} %all-reduce.1, s32[1024]{0:T(1024)S(1)} %pad_clamp_fusion), kind=kCustom, calls=%fused_computation | custom fusion | bytes 4608 | tf_op jit(solution)/shard_map/jit(_take)/gather | solution.py:126
  35.8 0.1 reshape.85
  35.9 0.1 compare_reduce_fusion
  36.0 0.1 fusion
  36.1 0.1 reshape.82
  36.2 0.1 copy.65
  36.3 0.8 sort.34
  37.1 0.1 copy.67
  37.2 0.8 sort.35
  38.0 0.1 copy.66
  38.1 0.1 stack.17
  38.2 0.1 reshape.92
  38.3 2.9 %gather_fusion.1 = s32[384]{0:T(512)S(1)} fusion(s32[12,32]{1,0:T(8,128)S(1)} %get-tuple-element.14, s32[384]{0:T(512)S(1)} %reshape.92), kind=kCustom, calls=%fused_computation.1 | custom fusion | bytes 6144 | tf_op jit(solution)/shard_map/jit(take_along_axis)/gather | solution.py:130
  41.1 0.1 reshape.95
  41.2 0.1 select_n.48
  41.3 0.1 slice_compare_fusion
  41.4 0.1 pad_convert_fusion
  41.5 0.1 reshape.83
  41.5 0.6 stack.20.table_ref
  42.2 46.1 %collective-permute-done.5.refs_3_ = bf16[12,8,128,128]{3,2,1,0:T(8,128)(2,1)S(1)} collective-permute-done((bf16[12,8,128,128]{3,2,1,0:T(8,128)(2,1)}, bf16[12,8,128,128]{3,2,1,0:T(8,128)(2,1)S(1)}, u32[]{:S(2)}, u32[]{:S(2)}) %collective-permute-start.5) | collective-permute-done | bytes 3145760 | tf_op jit(solution)/shard_map/ppermute | solution.py:113
  88.3 0.0 copy-start
  88.3 64.7 %collective-permute-done.4.refs_2_ = bf16[12,8,128,128]{3,2,1,0:T(8,128)(2,1)} collective-permute-done((bf16[12,8,128,128]{3,2,1,0:T(8,128)(2,1)}, bf16[12,8,128,128]{3,2,1,0:T(8,128)(2,1)}, u32[]{:S(2)}, u32[]{:S(2)}) %collective-permute-start.4) | collective-permute-done | bytes 3145760 | tf_op jit(solution)/shard_map/ppermute | solution.py:113
  152.9 0.1 collective-permute-done.3.refs_1_
  153.1 9.9 %all-gather.2.cloned.1.call-done = bf16[512,1,128,128]{3,2,1,0:T(8,128)(2,1)} async-done(((bf16[64,1,128,128]{3,2,1,0:T(8,128)(2,1)}), bf16[512,1,128,128]{3,2,1,0:T(8,128)(2,1)}) %all-gather.2.cloned.1.call-update) | async-done | bytes 16777232 | tf_op jit(solution)/shard_map/all_gather | solution.py:121
  162.9 0.0 copy-done
  162.9 16.4 %shard_map.55 = bf16[12,4,128,128]{3,2,1,0:T(8,128)(2,1)} custom-call(s32[5,384]{1,0:T(8,128)} %stack.20.table_ref, bf16[12,8,128,128]{3,2,1,0:T(8,128)(2,1)} %refs_0_, bf16[12,8,128,128]{3,2,1,0:T(8,128)(2,1)} %collective-permute-done.3.refs_1_, bf16[12,8,128,128]{3,2,1,0:T(8,128)(2,1)} %collective-permute-done.4.refs_2_, ...), custom_call_target="tpu_custom_call" | custom-call | flops 1610612736 | bytes 26738688 | tf_op jit(solution)/shard_map/pallas_call | solution.py:100
  (9 shorter events, 0.1 us)
Async XLA Ops:
  6.5 156.4 %all-gather.2.cloned.1.call-start = ((), (), s32[]{:S(2)}) async-start(), calls=%async_computation | async-start | bytes 18874368 | tf_op jit(solution)/shard_map/all_gather | solution.py:121
  8.0 5.6 %collective-permute-start.2 = (s32[12,8]{1,0:T(8,128)S(1)}, s32[12,8]{1,0:T(8,128)S(1)}, u32[]{:S(2)}, u32[]{:S(2)}) collective-permute-start(s32[12,8]{1,0:T(8,128)S(1)} %copy.63), channel_id=1, source_target_pairs={{0,24},{8,16},{16,8},{24,0},{1,25},{9,17},{17,9},{25,1},{2,26},{10... | collective-permute-start | bytes 1160 | tf_op jit(solution)/shard_map/ppermute | solution.py:113
  11.9 3.7 %collective-permute-start.1 = (s32[12,8]{1,0:T(8,128)S(1)}, s32[12,8]{1,0:T(8,128)S(1)}, u32[]{:S(2)}, u32[]{:S(2)}) collective-permute-start(s32[12,8]{1,0:T(8,128)S(1)} %copy.63), channel_id=1, source_target_pairs={{0,16},{8,24},{16,0},{24,8},{1,17},{9,25},{17,1},{25,9},{2,18},{10... | collective-permute-start | bytes 1160 | tf_op jit(solution)/shard_map/ppermute | solution.py:113
  12.5 3.7 %collective-permute-start = (s32[12,8]{1,0:T(8,128)S(1)}, s32[12,8]{1,0:T(8,128)S(1)}, u32[]{:S(2)}, u32[]{:S(2)}) collective-permute-start(s32[12,8]{1,0:T(8,128)S(1)} %copy.63), channel_id=1, source_target_pairs={{0,8},{8,0},{16,24},{24,16},{1,9},{9,1},{17,25},{25,17},{2,10},{10... | collective-permute-start | bytes 1160 | tf_op jit(solution)/shard_map/ppermute | solution.py:113
  16.2 72.1 %collective-permute-start.5 = (bf16[12,8,128,128]{3,2,1,0:T(8,128)(2,1)}, bf16[12,8,128,128]{3,2,1,0:T(8,128)(2,1)S(1)}, u32[]{:S(2)}, u32[]{:S(2)}) collective-permute-start(bf16[12,8,128,128]{3,2,1,0:T(8,128)(2,1)} %refs_0_), channel_id=1, source_target_pairs={{0,24},{8,16},{16,8},{24,0},{1,25},{9,17},{17,9},{25,1},{2,26},{10... | collective-permute-start | bytes 9437192 | tf_op jit(solution)/shard_map/ppermute | solution.py:113
  17.7 135.3 %collective-permute-start.4 = (bf16[12,8,128,128]{3,2,1,0:T(8,128)(2,1)}, bf16[12,8,128,128]{3,2,1,0:T(8,128)(2,1)}, u32[]{:S(2)}, u32[]{:S(2)}) collective-permute-start(bf16[12,8,128,128]{3,2,1,0:T(8,128)(2,1)} %refs_0_), channel_id=1, source_target_pairs={{0,16},{8,24},{16,0},{24,8},{1,17},{9,25},{17,1},{25,9},{2,18},{10... | collective-permute-start | bytes 9437192 | tf_op jit(solution)/shard_map/ppermute | solution.py:113
  17.8 135.3 %collective-permute-start.3 = (bf16[12,8,128,128]{3,2,1,0:T(8,128)(2,1)}, bf16[12,8,128,128]{3,2,1,0:T(8,128)(2,1)}, u32[]{:S(2)}, u32[]{:S(2)}) collective-permute-start(bf16[12,8,128,128]{3,2,1,0:T(8,128)(2,1)} %refs_0_), channel_id=1, source_target_pairs={{0,8},{8,0},{16,24},{24,16},{1,9},{9,1},{17,25},{25,17},{2,10},{10... | collective-permute-start | bytes 9437192 | tf_op jit(solution)/shard_map/ppermute | solution.py:113
  88.3 74.7 %copy-start = (bf16[12,8,128,128]{3,2,1,0:T(8,128)(2,1)}, bf16[12,8,128,128]{3,2,1,0:T(8,128)(2,1)S(1)}, u32[]{:S(2)}) copy-start(bf16[12,8,128,128]{3,2,1,0:T(8,128)(2,1)S(1)} %collective-permute-done.5.refs_3_) | copy-start | bytes 9437188
Sparse Core Ops, SparseCore 0:
  8.9 153.9 all-gather.1
